TPU v7x, 32 devices: a whole 2x2x4 slice. The times are simulated.
32 devices in a mesh: dp: 16 (over z, x, core), group: 2 (over y).
Axes of the slice: x: 2, y: 2, z: 4, core: 2. Of those that a mesh axis runs over, the one named last changes fastest.
Arguments:
- inputs: bfloat16 [32768, 2048], P('dp', 'group'), may hold values from -6 to 6
- grad_out: bfloat16 [32768, 2048], P(('dp', 'group')), may hold values from -0.0625 to 0.0625
- weight: bfloat16 [2048, 2048], P('group'), may hold values from -6 to 6
- old_basis: float32 [2048, 256], P('group'), may hold values from -0.125 to 0.125
- first_moment: float32 [256, 2048], P(None, 'dp'), may hold values from -6 to 6
- second_moment: float32 [256, 2048], P(None, 'dp'), may hold values from 0.1 to 3
Outputs:
- new_weight: bfloat16 [2048, 2048], P('group')
- new_first: float32 [256, 2048], P(None, 'dp')
- new_second: float32 [256, 2048], P(None, 'dp')
- new_basis: float32 [2048, 256], P('group')
All inputs are finite; a program needn't handle non-finite values.
Results may differ from a plain program's by a relative error of at most 0.011.
Values may be sent and summed in bfloat16 or wider, within the bound.
No kernel may reach another device: no remote copies, remote signals or barrier semaphores. Data moves between devices by JAX's collectives and lax.ppermute only.
A program may use at most 64 MiB of HBM per device.

v0:
```python
import jax
import jax.numpy as jnp
from jax import lax
from jax.sharding import PartitionSpec as P

NS_STEPS = 5
STEP = 10


BETA_ONE = 0.9
BETA_TWO = 0.99
ADAM_EPS = 1e-08
HIGHEST = lax.Precision.HIGHEST


def matmul(left, right):
    return jnp.dot(left, right, precision=HIGHEST)


def inner_gram(matrix):
    return lax.dot_general(matrix, matrix, (((0,), (0,)), ((), ())), precision=HIGHEST)


def refine_group(subspace):
    squares = lax.psum(jnp.sum(subspace * subspace), "group")
    iterate = subspace / jnp.sqrt(squares)
    for sweep in range(NS_STEPS):
        gram = lax.psum(inner_gram(iterate).astype(jnp.bfloat16), "group").astype(jnp.float32)
        iterate = 1.5 * iterate - 0.5 * matmul(iterate, gram)
    return iterate


def shards(inputs, grad_out, weight, old_basis, first_moment, second_moment):
    partial_grad = lax.dot_general(
        inputs,
        lax.all_gather(grad_out, "group", axis=0, tiled=True),
        (((0,), (0,)), ((), ())),
        preferred_element_type=jnp.float32,
    )
    grad_block = lax.psum_scatter(partial_grad, "dp", scatter_dimension=1, tiled=True)
    projected = lax.psum(matmul(old_basis.T, grad_block).astype(jnp.bfloat16), "group").astype(
        jnp.float32
    )
    new_first = BETA_ONE * first_moment + (1.0 - BETA_ONE) * projected
    new_second = BETA_TWO * second_moment + (1.0 - BETA_TWO) * projected * projected
    direction = (
        new_first
        / (1.0 - BETA_ONE**STEP)
        / (jnp.sqrt(new_second / (1.0 - BETA_TWO**STEP)) + ADAM_EPS)
    )
    col_count = grad_block.shape[1]
    col_offset = lax.axis_index("dp") * col_count
    own_cols = lax.dynamic_slice_in_dim(weight, col_offset, col_count, 1).astype(jnp.float32)
    updated = (own_cols - matmul(old_basis, direction)).astype(jnp.bfloat16)
    new_weight = lax.all_gather(updated, "dp", axis=1, tiled=True)
    subspace_terms = matmul(grad_block, projected.T)
    subspace = lax.psum(subspace_terms, "dp")
    new_basis = refine_group(subspace)
    return (new_weight, new_first, new_second, new_basis)


def solution(mesh):
    return jax.shard_map(
        shards,
        mesh=mesh,
        in_specs=(
            P("dp", "group"),
            P(("dp", "group"), None),
            P("group", None),
            P("group", None),
            P(None, "dp"),
            P(None, "dp"),
        ),
        out_specs=(P("group", None), P(None, "dp"), P(None, "dp"), P("group", None)),
        check_vma=False,
    )
```

profile of v0, /device:TPU:0, one launch (start us, length us, event | category | flops | bytes accessed | tf_op | source)
XLA Modules:
  0.0 558.3 jit_solution(406713574473706663)
XLA Ops:
  7.2 0.0 copy-start
  7.2 0.0 all-gather.3.cloned.1.call-start
  7.2 0.7 all-gather.3.cloned.1.call-update
  7.9 0.0 reduce-scatter.2.cloned.1.call-start
  8.0 108.3 %all-gather.3.cloned.1.call-done = bf16[2048,2048]{1,0:T(8,128)(2,1)} async-done(((bf16[1024,2048]{1,0:T(8,128)(2,1)}), bf16[2048,2048]{1,0:T(8,128)(2,1)}) %all-gather.3.cloned.1.call-update) | async-done | bytes 8388624 | tf_op jit(solution)/shard_map/all_gather | solution.py:36
  116.3 14.6 %fusion.21 = f32[1024,2048]{1,0:T(8,128)} fusion(bf16[2048,1024]{1,0:T(8,128)(2,1)} %param.6, bf16[2048,2048]{1,0:T(8,128)(2,1)} %all-gather.3.cloned.1.call-done), kind=kOutput, calls=%fused_computation.38 | convolution fusion | flops 8589934592 | bytes 20971520 | tf_op jit(solution)/shard_map/dot_general | solution.py:34
  130.9 0.0 reduce-scatter.2.cloned.1.call-update
  130.9 0.0 all-reduce.8.cloned.1.call-start
  130.9 103.7 %reduce-scatter.2.cloned.1.call-done = f32[1024,128]{1,0:T(8,128)} async-done(((f32[1024,2048]{1,0:T(8,128)}), f32[1024,128]{1,0:T(8,128)}) %reduce-scatter.2.cloned.1.call-update) | async-done | bytes 524304 | tf_op jit(solution)/shard_map/reduce_scatter | solution.py:40
  234.6 0.0 copy-done
  234.6 2.7 fusion.7
  237.4 0.0 all-reduce.8.cloned.1.call-update
  237.4 0.0 all-reduce.10.cloned.1.call-start
  237.4 20.7 %all-reduce.8.cloned.1.call-done = bf16[256,128]{0,1:T(8,128)(2,1)} async-done(((bf16[256,128]{0,1:T(8,128)(2,1)}), bf16[256,128]{0,1:T(8,128)(2,1)}) %all-reduce.8.cloned.1.call-update) | async-done | bytes 65552 | tf_op jit(solution)/shard_map/psum | solution.py:41
  258.1 2.6 fusion.22
  260.7 0.0 all-reduce.10.cloned.1.call-update
  260.7 0.0 all-reduce.12.cloned.1.call-start
  260.8 95.1 %all-reduce.10.cloned.1.call-done = f32[1024,256]{1,0:T(8,128)} async-done(((f32[1024,256]{1,0:T(8,128)}), f32[1024,256]{1,0:T(8,128)}) %all-reduce.10.cloned.1.call-update) | async-done | bytes 1048592 | tf_op jit(solution)/shard_map/psum | solution.py:57
  355.8 0.0 copy-start.1
  355.8 2.2 multiply_reduce_fusion
  358.0 5.5 psum.58
  364.3 4.0 convolution_convert_fusion.4
  368.3 0.0 all-reduce.12.cloned.1.call-update
  368.3 0.0 all-reduce.14.cloned.1.call-start
  368.4 20.7 %all-reduce.12.cloned.1.call-done = bf16[256,256]{1,0:T(8,128)(2,1)} async-done(((bf16[256,256]{1,0:T(8,128)(2,1)}), bf16[256,256]{1,0:T(8,128)(2,1)}) %all-reduce.12.cloned.1.call-update) | async-done | bytes 131088 | tf_op jit(solution)/shard_map/psum | solution.py:28
  389.1 0.0 copy-done.1
  389.1 1.6 fusion.4
  390.7 0.0 copy-start.2
  390.7 0.0 copy-start.3
  390.7 2.5 convolution_convert_fusion.3
  393.2 0.0 all-reduce.14.cloned.1.call-update
  393.2 0.2 all-reduce.16.cloned.1.call-start
  393.5 21.4 %all-reduce.14.cloned.1.call-done = bf16[256,256]{1,0:T(8,128)(2,1)} async-done(((bf16[256,256]{1,0:T(8,128)(2,1)}), bf16[256,256]{1,0:T(8,128)(2,1)}) %all-reduce.14.cloned.1.call-update) | async-done | bytes 131088 | tf_op jit(solution)/shard_map/psum | solution.py:28
  414.9 1.5 fusion.3
  416.4 2.5 convolution_convert_fusion.2
  418.9 0.0 all-reduce.16.cloned.1.call-update
  419.0 0.0 all-reduce.18.cloned.1.call-start
  419.0 1.0 constant_dynamic-slice_fusion
  420.0 0.9 copy.16
  420.8 0.0 copy-done.2
  420.8 0.1 copy.11
  420.9 0.0 copy-done.3
  421.0 0.8 copy.12
  421.7 18.9 %all-reduce.16.cloned.1.call-done = bf16[256,256]{1,0:T(8,128)(2,1)} async-done(((bf16[256,256]{1,0:T(8,128)(2,1)}), bf16[256,256]{1,0:T(8,128)(2,1)}) %all-reduce.16.cloned.1.call-update) | async-done | bytes 131088 | tf_op jit(solution)/shard_map/psum | solution.py:28
  440.6 1.5 fusion.2
  442.2 2.5 convolution_convert_fusion.1
  444.7 0.0 all-reduce.18.cloned.1.call-update
  444.7 0.0 all-reduce.20.cloned.1.call-start
  444.7 1.0 fusion.8
  445.7 20.6 %all-reduce.18.cloned.1.call-done = bf16[256,256]{1,0:T(8,128)(2,1)} async-done(((bf16[256,256]{1,0:T(8,128)(2,1)}), bf16[256,256]{1,0:T(8,128)(2,1)}) %all-reduce.18.cloned.1.call-update) | async-done | bytes 131088 | tf_op jit(solution)/shard_map/psum | solution.py:28
  466.4 1.5 fusion.1
  467.9 2.5 convolution_convert_fusion
  470.4 0.0 all-reduce.20.cloned.1.call-update
  470.4 0.0 all-gather.5.cloned.1.call-start
  470.5 2.9 fusion.6
  473.3 0.0 all-gather.5.cloned.1.call-update
  473.4 0.8 copy.14
  474.1 0.8 copy.15
  474.9 17.2 %all-reduce.20.cloned.1.call-done = bf16[256,256]{1,0:T(8,128)(2,1)} async-done(((bf16[256,256]{1,0:T(8,128)(2,1)}), bf16[256,256]{1,0:T(8,128)(2,1)}) %all-reduce.20.cloned.1.call-update) | async-done | bytes 131088 | tf_op jit(solution)/shard_map/psum | solution.py:28
  492.1 2.5 fusion
  494.6 50.5 %all-gather.5.cloned.1.call-done = bf16[1024,2048]{0,1:T(8,128)(2,1)} async-done(((bf16[1024,128]{0,1:T(8,128)(2,1)}), bf16[1024,2048]{0,1:T(8,128)(2,1)}) %all-gather.5.cloned.1.call-update) | async-done | bytes 4194320 | tf_op jit(solution)/shard_map/all_gather | solution.py:55
  545.1 6.4 %copy.13 = bf16[1024,2048]{1,0:T(8,128)(2,1)} copy(bf16[1024,2048]{0,1:T(8,128)(2,1)} %all-gather.5.cloned.1.call-done) | data formatting | bytes 8388608
Async XLA Ops:
  7.2 227.5 %copy-start = (f32[1024,256]{1,0:T(8,128)S(1)}, f32[1024,256]{1,0:T(8,128)}, u32[]{:S(2)}) copy-start(f32[1024,256]{1,0:T(8,128)} %param.9) | copy-start | bytes 3145732
  7.2 109.1 %all-gather.3.cloned.1.call-start = ((), (), s32[]{:S(2)}) async-start(), calls=%async_computation.1 | async-start | bytes 12582912 | tf_op jit(solution)/shard_map/all_gather | solution.py:36
  7.9 226.7 %reduce-scatter.2.cloned.1.call-start = ((), (), s32[]{:S(2)}) async-start(), calls=%async_computation.2 | async-start | bytes 8912896 | tf_op jit(solution)/shard_map/reduce_scatter | solution.py:40
  130.9 127.2 %all-reduce.8.cloned.1.call-start = ((), (), s32[]{:S(2)}) async-start(), calls=%async_computation.3 | async-start | bytes 131072 | tf_op jit(solution)/shard_map/psum | solution.py:41
  237.4 118.5 %all-reduce.10.cloned.1.call-start = ((), (), s32[]{:S(2)}) async-start(), calls=%async_computation.5 | async-start | bytes 2097152 | tf_op jit(solution)/shard_map/psum | solution.py:57
  260.7 128.4 %all-reduce.12.cloned.1.call-start = ((), (), s32[]{:S(2)}) async-start(), calls=%async_computation.6 | async-start | bytes 262144 | tf_op jit(solution)/shard_map/psum | solution.py:28
  355.8 33.3 %copy-start.1 = (f32[1024,256]{1,0:T(8,128)S(1)}, f32[1024,256]{1,0:T(8,128)}, u32[]{:S(2)}) copy-start(f32[1024,256]{1,0:T(8,128)} %all-reduce.10.cloned.1.call-done) | copy-start | bytes 3145732
  368.3 46.6 %all-reduce.14.cloned.1.call-start = ((), (), s32[]{:S(2)}) async-start(), calls=%async_computation.7 | async-start | bytes 262144 | tf_op jit(solution)/shard_map/psum | solution.py:28
  390.7 30.2 %copy-start.2 = (f32[256,128]{1,0:T(8,128)S(1)}, f32[256,128]{1,0:T(8,128)}, u32[]{:S(2)}) copy-start(f32[256,128]{1,0:T(8,128)} %param.10) | copy-start | bytes 393220
  390.7 30.3 %copy-start.3 = (f32[256,128]{1,0:T(8,128)S(1)}, f32[256,128]{1,0:T(8,128)}, u32[]{:S(2)}) copy-start(f32[256,128]{1,0:T(8,128)} %param.11) | copy-start | bytes 393220
  393.2 47.4 %all-reduce.16.cloned.1.call-start = ((), (), s32[]{:S(2)}) async-start(), calls=%async_computation.8 | async-start | bytes 262144 | tf_op jit(solution)/shard_map/psum | solution.py:28
  419.0 47.4 %all-reduce.18.cloned.1.call-start = ((), (), s32[]{:S(2)}) async-start(), calls=%async_computation.9 | async-start | bytes 262144 | tf_op jit(solution)/shard_map/psum | solution.py:28
  444.7 47.4 %all-reduce.20.cloned.1.call-start = ((), (), s32[]{:S(2)}) async-start(), calls=%async_computation.10 | async-start | bytes 262144 | tf_op jit(solution)/shard_map/psum | solution.py:28
  470.4 74.7 %all-gather.5.cloned.1.call-start = ((), (), s32[]{:S(2)}) async-start(), calls=%async_computation.4 | async-start | bytes 4456448 | tf_op jit(solution)/shard_map/all_gather | solution.py:55
Sparse Core Ops, SparseCore 0:
  9.5 106.6 all-gather.2
  131.0 103.5 reduce-scatter.1
  237.5 20.5 all-reduce.7
  262.0 93.7 all-reduce.9
  368.4 20.6 all-reduce.11
  393.4 21.5 all-reduce.13
  419.1 21.5 all-reduce.15
  444.8 21.5 all-reduce.17
  470.5 21.5 all-reduce.19
  494.7 50.3 all-gather.4
where the time goes:
time: 559 us; the launch traced here: 558 us
  waiting for transfers between devices  478 us (86%)
  matrix products  45.4 us (8%)
  between operations  15 us (3%)
  local copies, waits for them, and re-layouts  10.6 us (2%)
    all_gather x1, waiting for transfers between devices, shards(): lax.all_gather(grad_out, 'group', axis=0, tiled=True)  108 us
    reduce_scatter x1, waiting for transfers between devices, shards(): lax.psum_scatter(partial_grad, 'dp', scatter_dimension=1, tiled=True)  104 us
    psum x5, waiting for transfers between devices, refine_group(): lax.psum(inner_gram(iterate).astype(jnp.bfloat16), 'group')  99 us
    psum x1, waiting for transfers between devices, shards(): subspace = lax.psum(subspace_terms, 'dp')  95.1 us
    all_gather x1, waiting for transfers between devices, shards(): new_weight = lax.all_gather(updated, 'dp', axis=1, tiled=True)  50.5 us
    psum x1, waiting for transfers between devices, shards(): lax.psum(matmul(old_basis.T, grad_block).astype(jnp.bfloat16), 'group')  20.7 us
    dot_general x8, matrix products, matmul(): return jnp.dot(left, right, precision=HIGHEST)  16.8 us
    dot_general x1, matrix products, shards(): lax.dot_general(inputs, lax.all_gather(grad_out, 'group', axis=0, tiled=T...  14.6 us
  transfers between devices with their start and end apart: 10, of which 10 were waited for; matrix products, arithmetic and copies ran while one was open for 2% of the time, Pallas kernels for 0%

commit v1 on v0

v1 whole, which is shorter than its diff:
```python
import jax
import jax.numpy as jnp
from jax import lax
from jax.sharding import PartitionSpec as P

NS_STEPS = 5
STEP = 10


BETA_ONE = 0.9
BETA_TWO = 0.99
ADAM_EPS = 1e-08
HIGHEST = lax.Precision.HIGHEST
F32 = jnp.float32
BF16 = jnp.bfloat16


def matmul(left, right):
    return jnp.dot(left, right, precision=HIGHEST)


def split(value):
    high = value.astype(BF16)
    return high, (value - high.astype(F32)).astype(BF16)


def dot_mixed(left, right, dims):
    def one(a, b):
        return lax.dot_general(a, b, (dims, ((), ())), preferred_element_type=F32)

    if left.dtype == F32:
        high, low = split(left)
        return one(high, right) + one(low, right)
    high, low = split(right)
    return one(left, high) + one(left, low)


def log2(n):
    bits = n.bit_length() - 1
    assert 1 << bits == n
    return bits


def swap(x, axis, n, bit):
    return lax.ppermute(x, axis, [(k, k ^ (1 << bit)) for k in range(n)])


def reduce_scatter(x, axis, n, dim, order):
    levels = log2(n)
    me = lax.axis_index(axis)
    shape = x.shape
    block = shape[dim] // n
    x = x.reshape(shape[:dim] + (2,) * levels + (block,) + shape[dim + 1 :])
    remaining = list(range(levels - 1, -1, -1))
    for bit in order:
        pos = dim + remaining.index(bit)
        mine = (me >> bit) & 1
        keep = lax.dynamic_index_in_dim(x, mine, axis=pos, keepdims=False)
        send = lax.dynamic_index_in_dim(x, 1 - mine, axis=pos, keepdims=False)
        x = keep + swap(send, axis, n, bit)
        remaining.remove(bit)
    return x.reshape(shape[:dim] + (block,) + shape[dim + 1 :])


def all_gather(x, axis, n, dim, order):
    me = lax.axis_index(axis)
    shape = x.shape
    present = []
    for bit in order:
        other = swap(x, axis, n, bit)
        first = ((me >> bit) & 1) == 0
        low = jnp.where(first, x, other)
        high = jnp.where(first, other, x)
        present = sorted(present + [bit], reverse=True)
        x = jnp.stack([low, high], axis=dim + present.index(bit))
    return x.reshape(shape[:dim] + (n * shape[dim],) + shape[dim + 1 :])


def all_reduce(x, axis, n):
    for bit in range(log2(n)):
        x = x + swap(x, axis, n, bit)
    return x


def make_shards(dp_count, group_count):
    dp_up = list(range(log2(dp_count)))
    dp_down = dp_up[::-1]
    group_up = list(range(log2(group_count)))
    group_down = group_up[::-1]

    def shards(inputs, grad_out, weight, old_basis, first_moment, second_moment):
        basis_high, basis_low = split(old_basis)
        tokens_basis = lax.dot_general(
            inputs, basis_high, (((1,), (0,)), ((), ())), preferred_element_type=F32
        ) + lax.dot_general(inputs, basis_low, (((1,), (0,)), ((), ())), preferred_element_type=F32)
        tokens_basis = reduce_scatter(tokens_basis, "group", group_count, 0, group_up)
        projected_part = dot_mixed(tokens_basis, grad_out, ((0,), (0,)))
        projected = reduce_scatter(projected_part, "dp", dp_count, 1, dp_up)
        projected = all_reduce(projected, "group", group_count)

        new_first = BETA_ONE * first_moment + (1.0 - BETA_ONE) * projected
        new_second = BETA_TWO * second_moment + (1.0 - BETA_TWO) * projected * projected
        direction = (
            new_first
            / (1.0 - BETA_ONE**STEP)
            / (jnp.sqrt(new_second / (1.0 - BETA_TWO**STEP)) + ADAM_EPS)
        )

        projected_all = all_gather(projected, "dp", dp_count, 1, dp_down)
        direction_all = all_gather(direction, "dp", dp_count, 1, dp_down)

        tokens_sub = dot_mixed(grad_out, projected_all, ((1,), (1,)))
        tokens_sub = all_gather(tokens_sub, "group", group_count, 0, group_down)
        subspace_part = dot_mixed(inputs, tokens_sub, ((0,), (0,)))
        subspace = reduce_scatter(subspace_part, "dp", dp_count, 0, dp_up)
        subspace = all_gather(subspace, "dp", dp_count, 0, dp_down)

        gram = lax.dot_general(subspace, subspace, (((0,), (0,)), ((), ())), precision=HIGHEST)
        gram = all_reduce(gram, "group", group_count)
        squares = jnp.trace(gram)
        current = gram / squares
        eye = jnp.eye(gram.shape[0], dtype=F32)
        product = None
        for sweep in range(NS_STEPS):
            step = 1.5 * eye - 0.5 * current
            product = step if product is None else matmul(product, step)
            if sweep + 1 < NS_STEPS:
                current = matmul(step, matmul(current, step))
        new_basis = matmul(subspace / jnp.sqrt(squares), product)

        change = matmul(old_basis, direction_all)
        new_weight = (weight.astype(F32) - change).astype(BF16)
        return (new_weight, new_first, new_second, new_basis)

    return shards


def solution(mesh):
    return jax.shard_map(
        make_shards(mesh.shape["dp"], mesh.shape["group"]),
        mesh=mesh,
        in_specs=(
            P("dp", "group"),
            P(("dp", "group"), None),
            P("group", None),
            P("group", None),
            P(None, "dp"),
            P(None, "dp"),
        ),
        out_specs=(P("group", None), P(None, "dp"), P(None, "dp"), P("group", None)),
        check_vma=False,
    )
```

time: 559 us -> 238 us (0.43)
  waiting for transfers between devices: 478 us -> 131 us
  starting transfers between devices: 0.59 us -> 27.1 us
  local copies, waits for them, and re-layouts: 10.6 us -> 30.5 us
  between operations: 15 us -> 1.94 us
  matrix products: 45.4 us -> 37.2 us
  other arithmetic: 3.17 us -> 10.3 us
    psum x7 -> x0, waiting for transfers between devices: 215 us -> none  [the longest x5 99 us: refine_group(): lax.psum(inner_gram(iterate).astype(jnp.bfloat16), 'group')]
    all_gather x2 -> x0, waiting for transfers between devices: 159 us -> none  [the longest x1 108 us: shards(): lax.all_gather(grad_out, 'group', axis=0, tiled=True)]
    ppermute x0 -> x24, waiting for transfers between devices: none -> 131 us  [swap(): return lax.ppermute(x, axis, [(k, k ^ 1 << bit) for k in range(n)])]
    reduce_scatter x1 -> x0, waiting for transfers between devices: 104 us -> none  [shards(): lax.psum_scatter(partial_grad, 'dp', scatter_dimension=1, tiled=True)]
    ppermute x0 -> x24, starting transfers between devices: none -> 27.1 us  [swap(): return lax.ppermute(x, axis, [(k, k ^ 1 << bit) for k in range(n)])]
    unnamed x14 -> x26, local copies, waits for them, and re-layouts: 9.66 us -> 19.4 us
    dot_general x6 -> x9, matrix products: 28.6 us -> 19.9 us  [the longest x6 12.8 us: one(): return lax.dot_general(a, b, (dims, ((), ())), preferred_element_type=F32)]
    another operation x0 -> x25, other arithmetic: none -> 7.2 us  [all_gather(): x = jnp.stack([low, high], axis=dim + present.index(bit))]
  transfers between devices with their start and end apart: 10 -> 24, of which waited for: 10 -> 20; matrix products, arithmetic and copies ran while one was open for 2% -> 11% of each run, Pallas kernels for 0% -> 0%
where the time goes in v1:
time: 238 us
  waiting for transfers between devices  131 us (55%)
  matrix products  37.2 us (16%)
  local copies, waits for them, and re-layouts  30.5 us (13%)
  starting transfers between devices  27.1 us (11%)
  other arithmetic  10.3 us (4%)
    ppermute x24, waiting for transfers between devices, swap(): return lax.ppermute(x, axis, [(k, k ^ 1 << bit) for k in range(n)])  131 us
    ppermute x24, starting transfers between devices, swap(): return lax.ppermute(x, axis, [(k, k ^ 1 << bit) for k in range(n)])  27.1 us
    unnamed x26, local copies, waits for them, and re-layouts  19.4 us
    dot_general x14, matrix products, matmul(): return jnp.dot(left, right, precision=HIGHEST)  17.3 us
    dot_general x6, matrix products, one(): return lax.dot_general(a, b, (dims, ((), ())), preferred_element_type=F32)  12.8 us
    another operation x25, other arithmetic, all_gather(): x = jnp.stack([low, high], axis=dim + present.index(bit))  7.2 us
  transfers between devices with their start and end apart: 24, of which 20 were waited for; matrix products, arithmetic and copies ran while one was open for 11% of the time, Pallas kernels for 0%

profile of v1, /device:TPU:0, one launch (start us, length us, event | category | flops | bytes accessed | tf_op | source)
XLA Modules:
  0.0 237.7 jit_solution(1674284163709373881)
XLA Ops:
  0.7 3.9 %fusion.21 = f32[2048,256]{1,0:T(8,128)S(1)} fusion(bf16[2048,1024]{1,0:T(8,128)(2,1)} %param.6, f32[1024,256]{1,0:T(8,128)} %param.9), kind=kOutput, calls=%fused_computation.82 | convolution fusion | flops 1074003968 | bytes 7340032 | tf_op jit(solution)/shard_map/dot_general | solution.py:93
  4.7 1.3 fusion.1
  6.0 1.0 dynamic-slice_bitcast_fusion
  7.0 3.0 %collective-permute-start = (f32[1024,256]{1,0:T(8,128)}, f32[1024,256]{1,0:T(8,128)}, u32[]{:S(2)}, u32[]{:S(2)}) collective-permute-start(f32[1024,256]{1,0:T(8,128)} %dynamic-slice_bitcast_fusion), channel_id=1, source_target_pairs={{0,1},{1,0},{2,3},{3,2},{4,5},{5,4},{6,7},{7,6},{8,9},{9,8},{10,11... | collective-permute-start | bytes 3145736 | tf_op jit(solution)/shard_map/ppermute | solution.py:45
  10.0 23.5 %collective-permute-done = f32[1024,256]{1,0:T(8,128)} collective-permute-done((f32[1024,256]{1,0:T(8,128)}, f32[1024,256]{1,0:T(8,128)}, u32[]{:S(2)}, u32[]{:S(2)}) %collective-permute-start) | collective-permute-done | bytes 1048608 | tf_op jit(solution)/shard_map/ppermute | solution.py:45
  33.5 3.8 %fusion.8 = f32[256,2048]{1,0:T(8,128)S(1)} fusion(bf16[1024,2048]{1,0:T(8,128)(2,1)} %param.7, f32[1024,256]{1,0:T(8,128)} %collective-permute-done, f32[2,1024,256]{2,1,0:T(8,128)S(1)} %bitcast.178, s32[]{:T(128)S(6)} %select_n.196), kind=kOutput, calls=%fused_computation.41 | convolution fusion | flops 1075052544 | bytes 8388612 | tf_op jit(solution)/shard_map/dot_general | solution.py:29
  37.3 3.9 %convolution_add_fusion = f32[256,2048]{1,0:T(8,128)} fusion(f32[256,2048]{1,0:T(8,128)S(1)} %fusion.8, bf16[1024,2048]{1,0:T(8,128)(2,1)S(1)} %copy-done.3, f32[1024,256]{1,0:T(8,128)} %collective-permute-done, f32[2,1024,256]{2,1,0:T(8,128)S(1)} %bitcast.179, s32[]{:T(128)S(6)} %select_n.196), kind=kOutput, calls=%fused_computation.4 | convolution fusion | flops 1074790400 | bytes 10485764 | tf_op jit(solution)/shard_map/dot_general | solution.py:29
  41.2 3.0 %reshape.30 = f32[256,2,2,2,2,128]{5,4,3,2,1,0:T(2,128)S(1)} reshape(f32[256,2048]{1,0:T(8,128)} %convolution_add_fusion) | data formatting | bytes 4194304 | tf_op jit(solution)/shard_map/reshape | solution.py:53
  44.2 2.8 %constant_dynamic-slice_fusion.3 = (f32[256,2,2,2,1,128]{5,4,3,2,1,0:T(1,128)}, f32[256,2,2,2,1,128]{5,4,3,2,1,0:T(1,128)S(1)}) fusion(f32[256,2,2,2,2,128]{5,4,3,2,1,0:T(2,128)S(1)} %reshape.30, s32[]{:T(128)S(6)} %select_n.198, s32[]{:T(128)S(6)} %select_n.199), kind=kLoop, calls=%fused_computation.140 | loop fusion | bytes 4194312 | tf_op jit(solution)/shard_map/jit(dynamic_index_in_dim)/dynamic_slice | solution.py:58
  47.0 1.2 copy.68
  48.1 2.9 %collective-permute-done.1 = f32[256,2,2,2,128]{4,0,3,2,1:T(8,128)S(1)} collective-permute-done((f32[256,2,2,2,128]{4,0,3,2,1:T(8,128)}, f32[256,2,2,2,128]{4,0,3,2,1:T(8,128)S(1)}, u32[]{:S(2)}, u32[]{:S(2)}) %collective-permute-start.1) | collective-permute-done | bytes 1048608 | tf_op jit(solution)/shard_map/ppermute | solution.py:45
  51.0 1.0 copy-done.7
  52.0 1.4 bitcast_add_fusion
  53.5 1.8 collective-permute-start.2
  55.3 12.2 %collective-permute-done.2 = f32[256,2,2,128]{3,0,2,1:T(8,128)S(1)} collective-permute-done((f32[256,2,2,128]{3,0,2,1:T(8,128)S(1)}, f32[256,2,2,128]{3,0,2,1:T(8,128)S(1)}, u32[]{:S(2)}, u32[]{:S(2)}) %collective-permute-start.2) | collective-permute-done | bytes 524320 | tf_op jit(solution)/shard_map/ppermute | solution.py:45
  67.6 1.9 collective-permute-start.3
  69.5 5.8 %collective-permute-done.3 = f32[256,2,128]{2,0,1:T(8,128)S(1)} collective-permute-done((f32[256,2,128]{2,0,1:T(8,128)S(1)}, f32[256,2,128]{2,0,1:T(8,128)S(1)}, u32[]{:S(2)}, u32[]{:S(2)}) %collective-permute-start.3) | collective-permute-done | bytes 262176 | tf_op jit(solution)/shard_map/ppermute | solution.py:45
  75.4 2.8 %collective-permute-start.4 = (f32[256,128]{0,1:T(8,128)S(1)}, f32[256,128]{0,1:T(8,128)S(1)}, u32[]{:S(2)}, u32[]{:S(2)}) collective-permute-start(f32[256,128]{0,1:T(8,128)S(1)} %bitcast.183), channel_id=1, source_target_pairs={{0,16},{2,18},{4,20},{6,22},{8,24},{10,26},{12,28},{14,30},{16,0},... | collective-permute-start | bytes 393224 | tf_op jit(solution)/shard_map/ppermute | solution.py:45
  78.3 4.8 %collective-permute-done.4 = f32[256,128]{0,1:T(8,128)S(1)} collective-permute-done((f32[256,128]{0,1:T(8,128)S(1)}, f32[256,128]{0,1:T(8,128)S(1)}, u32[]{:S(2)}, u32[]{:S(2)}) %collective-permute-start.4) | collective-permute-done | bytes 131104 | tf_op jit(solution)/shard_map/ppermute | solution.py:45
  83.1 1.6 collective-permute-start.5
  85.0 3.2 %collective-permute-done.5 = f32[256,128]{0,1:T(8,128)S(1)} collective-permute-done((f32[256,128]{0,1:T(8,128)S(1)}, f32[256,128]{0,1:T(8,128)S(1)}, u32[]{:S(2)}, u32[]{:S(2)}) %collective-permute-start.5) | collective-permute-done | bytes 131104 | tf_op jit(solution)/shard_map/ppermute | solution.py:45
  88.3 1.1 collective-permute-start.10
  89.4 6.3 %collective-permute-done.10 = f32[256,128]{0,1:T(8,128)S(1)} collective-permute-done((f32[256,128]{0,1:T(8,128)S(1)}, f32[256,128]{0,1:T(8,128)S(1)}, u32[]{:S(2)}, u32[]{:S(2)}) %collective-permute-start.10) | collective-permute-done | bytes 131104 | tf_op jit(solution)/shard_map/ppermute | solution.py:45
  95.8 6.4 %collective-permute-done.11 = f32[256,2,128]{0,2,1:T(8,128)S(1)} collective-permute-done((f32[256,2,128]{0,2,1:T(8,128)S(1)}, f32[256,2,128]{0,2,1:T(8,128)S(1)}, u32[]{:S(2)}, u32[]{:S(2)}) %collective-permute-start.11) | collective-permute-done | bytes 262176 | tf_op jit(solution)/shard_map/ppermute | solution.py:45
  102.3 1.6 collective-permute-start.12
  103.9 7.6 %collective-permute-done.12 = f32[256,2,2,128]{0,3,2,1:T(8,128)S(1)} collective-permute-done((f32[256,2,2,128]{0,3,2,1:T(8,128)S(1)}, f32[256,2,2,128]{0,3,2,1:T(8,128)S(1)}, u32[]{:S(2)}, u32[]{:S(2)}) %collective-permute-start.12) | collective-permute-done | bytes 524320 | tf_op jit(solution)/shard_map/ppermute | solution.py:45
  111.6 1.1 pad_maximum_fusion.4
  112.7 2.9 %collective-permute-done.13 = f32[256,2,2,2,128]{0,4,3,2,1:T(8,128)S(1)} collective-permute-done((f32[256,2,2,2,128]{0,4,3,2,1:T(8,128)}, f32[256,2,2,2,128]{0,4,3,2,1:T(8,128)S(1)}, u32[]{:S(2)}, u32[]{:S(2)}) %collective-permute-start.13) | collective-permute-done | bytes 1048608 | tf_op jit(solution)/shard_map/ppermute | solution.py:45
  116.4 1.9 copy-done.4
  118.3 1.3 fusion.96
  119.7 1.3 fusion.5
  121.0 1.6 collective-permute-start.14
  122.6 23.6 %collective-permute-done.14 = f32[1024,256]{0,1:T(8,128)S(1)} collective-permute-done((f32[1024,256]{0,1:T(8,128)S(1)}, f32[1024,256]{0,1:T(8,128)S(1)}, u32[]{:S(2)}, u32[]{:S(2)}) %collective-permute-start.14) | collective-permute-done | bytes 1048608 | tf_op jit(solution)/shard_map/ppermute | solution.py:45
  146.5 1.5 pad_maximum_fusion.2
  147.9 2.1 copy.56
  150.3 1.9 copy-done.2
  152.3 1.3 fusion.97
  153.5 1.3 fusion.4
  155.3 1.3 collective-permute-start.6
  157.3 1.6 collective-permute-start.16
  158.9 6.0 %collective-permute-done.6 = f32[256,128]{0,1:T(8,128)S(1)} collective-permute-done((f32[256,128]{0,1:T(8,128)S(1)}, f32[256,128]{0,1:T(8,128)S(1)}, u32[]{:S(2)}, u32[]{:S(2)}) %collective-permute-start.6) | collective-permute-done | bytes 131104 | tf_op jit(solution)/shard_map/ppermute | solution.py:45
  165.8 1.6 collective-permute-start.17
  167.4 6.8 %collective-permute-done.7 = f32[256,2,128]{0,2,1:T(8,128)S(1)} collective-permute-done((f32[256,2,128]{0,2,1:T(8,128)S(1)}, f32[256,2,128]{0,2,1:T(8,128)S(1)}, u32[]{:S(2)}, u32[]{:S(2)}) %collective-permute-start.7) | collective-permute-done | bytes 262176 | tf_op jit(solution)/shard_map/ppermute | solution.py:45
  174.3 1.6 collective-permute-start.8
  175.9 1.2 collective-permute-start.18
  177.1 4.4 %collective-permute-done.18 = f32[64,256]{1,0:T(8,128)S(1)} collective-permute-done((f32[64,256]{1,0:T(8,128)S(1)}, f32[64,256]{1,0:T(8,128)S(1)}, u32[]{:S(2)}, u32[]{:S(2)}) %collective-permute-start.18) | collective-permute-done | bytes 65568 | tf_op jit(solution)/shard_map/ppermute | solution.py:45
  181.6 0.8 collective-permute-start.19
  182.4 3.6 %collective-permute-done.8 = f32[256,2,2,128]{0,3,2,1:T(8,128)S(1)} collective-permute-done((f32[256,2,2,128]{0,3,2,1:T(8,128)S(1)}, f32[256,2,2,128]{0,3,2,1:T(8,128)S(1)}, u32[]{:S(2)}, u32[]{:S(2)}) %collective-permute-start.8) | collective-permute-done | bytes 524320 | tf_op jit(solution)/shard_map/ppermute | solution.py:45
  186.1 0.8 collective-permute-done.19
  187.0 1.1 pad_maximum_fusion.3
  188.1 3.9 %collective-permute-done.20 = f32[2,64,256]{2,1,0:T(8,128)S(1)} collective-permute-done((f32[2,64,256]{2,1,0:T(8,128)S(1)}, f32[2,64,256]{2,1,0:T(8,128)S(1)}, u32[]{:S(2)}, u32[]{:S(2)}) %collective-permute-start.20) | collective-permute-done | bytes 131104 | tf_op jit(solution)/shard_map/ppermute | solution.py:45
  192.0 1.6 collective-permute-start.21
  193.6 4.9 %collective-permute-done.21 = f32[2,2,64,256]{3,2,1,0:T(8,128)S(1)} collective-permute-done((f32[2,2,64,256]{3,2,1,0:T(8,128)S(1)}, f32[2,2,64,256]{3,2,1,0:T(8,128)S(1)}, u32[]{:S(2)}, u32[]{:S(2)}) %collective-permute-start.21) | collective-permute-done | bytes 262176 | tf_op jit(solution)/shard_map/ppermute | solution.py:45
  198.5 0.9 pad_maximum_fusion.9
  199.4 6.4 %copy.40 = bf16[1024,2048]{0,1:T(8,128)(2,1)} copy(bf16[1024,2048]{1,0:T(8,128)(2,1)} %param.8) | data formatting | bytes 8388608 | tf_op args[2]
  207.3 1.4 select_bitcast_fusion.5
  209.0 1.8 convolution_bitcast_fusion.1
  210.8 1.6 collective-permute-start.23
  212.4 8.6 %fusion = bf16[1024,2048]{0,1:T(8,128)(2,1)} fusion(bf16[1024,2048]{0,1:T(8,128)(2,1)S(1)} %copy-done, f32[256,2048]{0,1:T(8,128)S(1)} %bitcast.176, f32[1024,256]{1,0:T(8,128)S(1)} %copy-done.5), kind=kOutput, calls=%fused_computation.1 | convolution fusion | flops 6448742400 | bytes 11534336 | tf_op jit(solution)/shard_map/dot_general | solution.py:19
  221.0 6.4 %copy.61 = bf16[1024,2048]{1,0:T(8,128)(2,1)} copy(bf16[1024,2048]{0,1:T(8,128)(2,1)} %fusion) | data formatting | bytes 8388608
  228.8 1.1 fusion.14
  229.8 1.0 fusion.13
  230.9 1.1 fusion.12
  235.8 2.0 fusion.99
  (87 shorter events, 10.8 us)
Async XLA Ops:
  0.6 4.0 %copy-start.1 = (bf16[2048,1024]{1,0:T(8,128)(2,1)S(1)}, bf16[2048,1024]{1,0:T(8,128)(2,1)}, u32[]{:S(2)}) copy-start(bf16[2048,1024]{1,0:T(8,128)(2,1)} %param.6) | copy-start | bytes 12582916
  0.6 4.0 %copy-start.5 = (f32[1024,256]{1,0:T(8,128)S(1)}, f32[1024,256]{1,0:T(8,128)}, u32[]{:S(2)}) copy-start(f32[1024,256]{1,0:T(8,128)} %param.9) | copy-start | bytes 3145732
  7.0 26.5 %collective-permute-start = (f32[1024,256]{1,0:T(8,128)}, f32[1024,256]{1,0:T(8,128)}, u32[]{:S(2)}, u32[]{:S(2)}) collective-permute-start(f32[1024,256]{1,0:T(8,128)} %dynamic-slice_bitcast_fusion), channel_id=1, source_target_pairs={{0,1},{1,0},{2,3},{3,2},{4,5},{5,4},{6,7},{7,6},{8,9},{9,8},{10,11... | collective-permute-start | bytes 3145736 | tf_op jit(solution)/shard_map/ppermute | solution.py:45
  10.0 27.3 %copy-start.3 = (bf16[1024,2048]{1,0:T(8,128)(2,1)S(1)}, bf16[1024,2048]{1,0:T(8,128)(2,1)}, u32[]{:S(2)}) copy-start(bf16[1024,2048]{1,0:T(8,128)(2,1)} %param.7) | copy-start | bytes 12582916
  47.0 5.0 %copy-start.6 = (f32[256,2,2,2,1,128]{5,4,3,2,1,0:T(1,128)S(1)}, f32[256,2,2,2,1,128]{5,4,3,2,1,0:T(1,128)}, u32[]{:S(2)}) copy-start(f32[256,2,2,2,1,128]{5,4,3,2,1,0:T(1,128)} %get-tuple-element.32) | copy-start | bytes 3145732
  48.1 2.9 %collective-permute-start.1 = (f32[256,2,2,2,128]{4,0,3,2,1:T(8,128)}, f32[256,2,2,2,128]{4,0,3,2,1:T(8,128)S(1)}, u32[]{:S(2)}, u32[]{:S(2)}) collective-permute-start(f32[256,2,2,2,128]{4,0,3,2,1:T(8,128)} %bitcast.175), channel_id=1, source_target_pairs={{0,2},{2,0},{4,6},{6,4},{8,10},{10,8},{12,14},{14,12},{16,18},{18,... | collective-permute-start | bytes 3145736 | tf_op jit(solution)/shard_map/ppermute | solution.py:45
  51.0 1.0 copy-start.7
  53.5 14.0 %collective-permute-start.2 = (f32[256,2,2,128]{3,0,2,1:T(8,128)S(1)}, f32[256,2,2,128]{3,0,2,1:T(8,128)S(1)}, u32[]{:S(2)}, u32[]{:S(2)}) collective-permute-start(f32[256,2,2,128]{3,0,2,1:T(8,128)S(1)} %dynamic-slice_bitcast_fusion.2), channel_id=1, source_target_pairs={{0,4},{2,6},{4,0},{6,2},{8,12},{10,14},{12,8},{14,10},{16,20},{18,... | collective-permute-start | bytes 1572872 | tf_op jit(solution)/shard_map/ppermute | solution.py:45
  55.3 29.5 %copy-start.8 = (f32[256,128]{1,0:T(8,128)S(1)}, f32[256,128]{1,0:T(8,128)}, u32[]{:S(2)}) copy-start(f32[256,128]{1,0:T(8,128)} %param.10) | copy-start | bytes 393220
  55.3 29.6 %copy-start.9 = (f32[256,128]{1,0:T(8,128)S(1)}, f32[256,128]{1,0:T(8,128)}, u32[]{:S(2)}) copy-start(f32[256,128]{1,0:T(8,128)} %param.11) | copy-start | bytes 393220
  67.6 7.6 %collective-permute-start.3 = (f32[256,2,128]{2,0,1:T(8,128)S(1)}, f32[256,2,128]{2,0,1:T(8,128)S(1)}, u32[]{:S(2)}, u32[]{:S(2)}) collective-permute-start(f32[256,2,128]{2,0,1:T(8,128)S(1)} %dynamic-slice_bitcast_fusion.4), channel_id=1, source_target_pairs={{0,8},{2,10},{4,12},{6,14},{8,0},{10,2},{12,4},{14,6},{16,24},{18,... | collective-permute-start | bytes 786440 | tf_op jit(solution)/shard_map/ppermute | solution.py:45
  75.4 7.7 %collective-permute-start.4 = (f32[256,128]{0,1:T(8,128)S(1)}, f32[256,128]{0,1:T(8,128)S(1)}, u32[]{:S(2)}, u32[]{:S(2)}) collective-permute-start(f32[256,128]{0,1:T(8,128)S(1)} %bitcast.183), channel_id=1, source_target_pairs={{0,16},{2,18},{4,20},{6,22},{8,24},{10,26},{12,28},{14,30},{16,0},... | collective-permute-start | bytes 393224 | tf_op jit(solution)/shard_map/ppermute | solution.py:45
  83.1 5.0 %collective-permute-start.5 = (f32[256,128]{0,1:T(8,128)S(1)}, f32[256,128]{0,1:T(8,128)S(1)}, u32[]{:S(2)}, u32[]{:S(2)}) collective-permute-start(f32[256,128]{0,1:T(8,128)S(1)} %bitcast_add_fusion.8), channel_id=1, source_target_pairs={{0,1},{1,0},{2,3},{3,2},{4,5},{5,4},{6,7},{7,6},{8,9},{9,8},{10,11... | collective-permute-start | bytes 393224 | tf_op jit(solution)/shard_map/ppermute | solution.py:45
  88.3 7.4 %collective-permute-start.10 = (f32[256,128]{0,1:T(8,128)S(1)}, f32[256,128]{0,1:T(8,128)S(1)}, u32[]{:S(2)}, u32[]{:S(2)}) collective-permute-start(f32[256,128]{0,1:T(8,128)S(1)} %get-tuple-element.25), channel_id=1, source_target_pairs={{0,16},{2,18},{4,20},{6,22},{8,24},{10,26},{12,28},{14,30},{16,0},... | collective-permute-start | bytes 393224 | tf_op jit(solution)/shard_map/ppermute | solution.py:45
  95.8 6.4 %collective-permute-start.11 = (f32[256,2,128]{0,2,1:T(8,128)S(1)}, f32[256,2,128]{0,2,1:T(8,128)S(1)}, u32[]{:S(2)}, u32[]{:S(2)}) collective-permute-start(f32[256,2,128]{0,2,1:T(8,128)S(1)} %pad_maximum_fusion.11), channel_id=1, source_target_pairs={{0,8},{2,10},{4,12},{6,14},{8,0},{10,2},{12,4},{14,6},{16,24},{18,... | collective-permute-start | bytes 786440 | tf_op jit(solution)/shard_map/ppermute | solution.py:45
  102.3 9.2 %collective-permute-start.12 = (f32[256,2,2,128]{0,3,2,1:T(8,128)S(1)}, f32[256,2,2,128]{0,3,2,1:T(8,128)S(1)}, u32[]{:S(2)}, u32[]{:S(2)}) collective-permute-start(f32[256,2,2,128]{0,3,2,1:T(8,128)S(1)} %pad_maximum_fusion.8), channel_id=1, source_target_pairs={{0,4},{2,6},{4,0},{6,2},{8,12},{10,14},{12,8},{14,10},{16,20},{18,... | collective-permute-start | bytes 1572872 | tf_op jit(solution)/shard_map/ppermute | solution.py:45
  112.7 2.9 %collective-permute-start.13 = (f32[256,2,2,2,128]{0,4,3,2,1:T(8,128)}, f32[256,2,2,2,128]{0,4,3,2,1:T(8,128)S(1)}, u32[]{:S(2)}, u32[]{:S(2)}) collective-permute-start(f32[256,2,2,2,128]{0,4,3,2,1:T(8,128)} %pad_maximum_fusion.4), channel_id=1, source_target_pairs={{0,2},{2,0},{4,6},{6,4},{8,10},{10,8},{12,14},{14,12},{16,18},{18,... | collective-permute-start | bytes 3145736 | tf_op jit(solution)/shard_map/ppermute | solution.py:45
  116.1 2.2 copy-start.4
  121.0 25.3 %collective-permute-start.14 = (f32[1024,256]{0,1:T(8,128)S(1)}, f32[1024,256]{0,1:T(8,128)S(1)}, u32[]{:S(2)}, u32[]{:S(2)}) collective-permute-start(f32[1024,256]{0,1:T(8,128)S(1)} %fusion.5), channel_id=1, source_target_pairs={{0,1},{1,0},{2,3},{3,2},{4,5},{5,4},{6,7},{7,6},{8,9},{9,8},{10,11... | collective-permute-start | bytes 3145736 | tf_op jit(solution)/shard_map/ppermute | solution.py:45
  150.1 2.2 copy-start.2
  155.2 2.0 collective-permute-start.15
  155.3 9.6 %collective-permute-start.6 = (f32[256,128]{0,1:T(8,128)S(1)}, f32[256,128]{0,1:T(8,128)S(1)}, u32[]{:S(2)}, u32[]{:S(2)}) collective-permute-start(f32[256,128]{0,1:T(8,128)S(1)} %get-tuple-element.22), channel_id=1, source_target_pairs={{0,16},{2,18},{4,20},{6,22},{8,24},{10,26},{12,28},{14,30},{16,0},... | collective-permute-start | bytes 393224 | tf_op jit(solution)/shard_map/ppermute | solution.py:45
  157.3 8.4 %collective-permute-start.16 = (f32[2,2,64,256]{3,2,1,0:T(8,128)S(1)}, f32[2,2,64,256]{3,2,1,0:T(8,128)S(1)}, u32[]{:S(2)}, u32[]{:S(2)}) collective-permute-start(f32[2,2,64,256]{3,2,1,0:T(8,128)S(1)} %dynamic-slice_bitcast_fusion.3), channel_id=1, source_target_pairs={{0,4},{2,6},{4,0},{6,2},{8,12},{10,14},{12,8},{14,10},{16,20},{18,... | collective-permute-start | bytes 786440 | tf_op jit(solution)/shard_map/ppermute | solution.py:45
  164.9 9.2 %collective-permute-start.7 = (f32[256,2,128]{0,2,1:T(8,128)S(1)}, f32[256,2,128]{0,2,1:T(8,128)S(1)}, u32[]{:S(2)}, u32[]{:S(2)}) collective-permute-start(f32[256,2,128]{0,2,1:T(8,128)S(1)} %pad_maximum_fusion.10), channel_id=1, source_target_pairs={{0,8},{2,10},{4,12},{6,14},{8,0},{10,2},{12,4},{14,6},{16,24},{18,... | collective-permute-start | bytes 786440 | tf_op jit(solution)/shard_map/ppermute | solution.py:45
  165.8 10.1 %collective-permute-start.17 = (f32[2,64,256]{2,1,0:T(8,128)S(1)}, f32[2,64,256]{2,1,0:T(8,128)S(1)}, u32[]{:S(2)}, u32[]{:S(2)}) collective-permute-start(f32[2,64,256]{2,1,0:T(8,128)S(1)} %dynamic-slice_bitcast_fusion.5), channel_id=1, source_target_pairs={{0,8},{2,10},{4,12},{6,14},{8,0},{10,2},{12,4},{14,6},{16,24},{18,... | collective-permute-start | bytes 393224 | tf_op jit(solution)/shard_map/ppermute | solution.py:45
  174.3 11.7 %collective-permute-start.8 = (f32[256,2,2,128]{0,3,2,1:T(8,128)S(1)}, f32[256,2,2,128]{0,3,2,1:T(8,128)S(1)}, u32[]{:S(2)}, u32[]{:S(2)}) collective-permute-start(f32[256,2,2,128]{0,3,2,1:T(8,128)S(1)} %pad_maximum_fusion.7), channel_id=1, source_target_pairs={{0,4},{2,6},{4,0},{6,2},{8,12},{10,14},{12,8},{14,10},{16,20},{18,... | collective-permute-start | bytes 1572872 | tf_op jit(solution)/shard_map/ppermute | solution.py:45
  175.9 5.6 %collective-permute-start.18 = (f32[64,256]{1,0:T(8,128)S(1)}, f32[64,256]{1,0:T(8,128)S(1)}, u32[]{:S(2)}, u32[]{:S(2)}) collective-permute-start(f32[64,256]{1,0:T(8,128)S(1)} %dynamic-slice_bitcast_fusion.6), channel_id=1, source_target_pairs={{0,16},{2,18},{4,20},{6,22},{8,24},{10,26},{12,28},{14,30},{16,0},... | collective-permute-start | bytes 196616 | tf_op jit(solution)/shard_map/ppermute | solution.py:45
  181.6 5.3 %collective-permute-start.19 = (f32[64,256]{1,0:T(8,128)S(1)}, f32[64,256]{1,0:T(8,128)S(1)}, u32[]{:S(2)}, u32[]{:S(2)}) collective-permute-start(f32[64,256]{1,0:T(8,128)S(1)} %bitcast_add_fusion.9), channel_id=1, source_target_pairs={{0,16},{2,18},{4,20},{6,22},{8,24},{10,26},{12,28},{14,30},{16,0},... | collective-permute-start | bytes 196616 | tf_op jit(solution)/shard_map/ppermute | solution.py:45
  186.9 5.0 %collective-permute-start.20 = (f32[2,64,256]{2,1,0:T(8,128)S(1)}, f32[2,64,256]{2,1,0:T(8,128)S(1)}, u32[]{:S(2)}, u32[]{:S(2)}) collective-permute-start(f32[2,64,256]{2,1,0:T(8,128)S(1)} %pad_maximum_fusion.13), channel_id=1, source_target_pairs={{0,8},{2,10},{4,12},{6,14},{8,0},{10,2},{12,4},{14,6},{16,24},{18,... | collective-permute-start | bytes 393224 | tf_op jit(solution)/shard_map/ppermute | solution.py:45
  188.1 19.2 %collective-permute-start.9 = (f32[256,2,2,2,128]{0,4,3,2,1:T(8,128)}, f32[256,2,2,2,128]{0,4,3,2,1:T(8,128)}, u32[]{:S(2)}, u32[]{:S(2)}) collective-permute-start(f32[256,2,2,2,128]{0,4,3,2,1:T(8,128)} %pad_maximum_fusion.3), channel_id=1, source_target_pairs={{0,2},{2,0},{4,6},{6,4},{8,10},{10,8},{12,14},{14,12},{16,18},{18,... | collective-permute-start | bytes 3145736 | tf_op jit(solution)/shard_map/ppermute | solution.py:45
  192.0 6.4 %collective-permute-start.21 = (f32[2,2,64,256]{3,2,1,0:T(8,128)S(1)}, f32[2,2,64,256]{3,2,1,0:T(8,128)S(1)}, u32[]{:S(2)}, u32[]{:S(2)}) collective-permute-start(f32[2,2,64,256]{3,2,1,0:T(8,128)S(1)} %pad_maximum_fusion.12), channel_id=1, source_target_pairs={{0,4},{2,6},{4,0},{6,2},{8,12},{10,14},{12,8},{14,10},{16,20},{18,... | collective-permute-start | bytes 786440 | tf_op jit(solution)/shard_map/ppermute | solution.py:45
  199.4 9.5 %collective-permute-start.22 = (f32[2,2,2,64,256]{4,3,2,1,0:T(8,128)}, f32[2,2,2,64,256]{4,3,2,1,0:T(8,128)S(1)}, u32[]{:S(2)}, u32[]{:S(2)}) collective-permute-start(f32[2,2,2,64,256]{4,3,2,1,0:T(8,128)} %pad_maximum_fusion.9), channel_id=1, source_target_pairs={{0,2},{2,0},{4,6},{6,4},{8,10},{10,8},{12,14},{14,12},{16,18},{18,... | collective-permute-start | bytes 1572872 | tf_op jit(solution)/shard_map/ppermute | solution.py:45
  208.7 3.7 %copy-start = (bf16[1024,2048]{0,1:T(8,128)(2,1)S(1)}, bf16[1024,2048]{0,1:T(8,128)(2,1)}, u32[]{:S(2)}) copy-start(bf16[1024,2048]{0,1:T(8,128)(2,1)} %copy.40) | copy-start | bytes 12582916
  210.8 16.6 %collective-permute-start.23 = (f32[256,256]{1,0:T(8,128)S(1)}, f32[256,256]{1,0:T(8,128)S(1)}, u32[]{:S(2)}, u32[]{:S(2)}) collective-permute-start(f32[256,256]{1,0:T(8,128)S(1)} %convolution_bitcast_fusion.1), channel_id=1, source_target_pairs={{0,1},{1,0},{2,3},{3,2},{4,5},{5,4},{6,7},{7,6},{8,9},{9,8},{10,11... | collective-permute-start | bytes 786440 | tf_op jit(solution)/shard_map/ppermute | solution.py:45

commit v2 on v1

--- a/solution.py
+++ b/solution.py
@@ -93,7 +93,9 @@
         tokens_basis = lax.dot_general(
             inputs, basis_high, (((1,), (0,)), ((), ())), preferred_element_type=F32
         ) + lax.dot_general(inputs, basis_low, (((1,), (0,)), ((), ())), preferred_element_type=F32)
-        tokens_basis = reduce_scatter(tokens_basis, "group", group_count, 0, group_up)
+        tokens_basis = reduce_scatter(
+            tokens_basis.astype(BF16), "group", group_count, 0, group_up
+        ).astype(F32)
         projected_part = dot_mixed(tokens_basis, grad_out, ((0,), (0,)))
         projected = reduce_scatter(projected_part, "dp", dp_count, 1, dp_up)
         projected = all_reduce(projected, "group", group_count)
@@ -107,10 +109,10 @@
         )
 
         projected_all = all_gather(projected, "dp", dp_count, 1, dp_down)
-        direction_all = all_gather(direction, "dp", dp_count, 1, dp_down)
+        direction_all = all_gather(direction.T, "dp", dp_count, 0, dp_down)
 
         tokens_sub = dot_mixed(grad_out, projected_all, ((1,), (1,)))
-        tokens_sub = all_gather(tokens_sub, "group", group_count, 0, group_down)
+        tokens_sub = all_gather(tokens_sub.astype(BF16), "group", group_count, 0, group_down)
         subspace_part = dot_mixed(inputs, tokens_sub, ((0,), (0,)))
         subspace = reduce_scatter(subspace_part, "dp", dp_count, 0, dp_up)
         subspace = all_gather(subspace, "dp", dp_count, 0, dp_down)
@@ -128,7 +130,13 @@
                 current = matmul(step, matmul(current, step))
         new_basis = matmul(subspace / jnp.sqrt(squares), product)
 
-        change = matmul(old_basis, direction_all)
+        direction_high, direction_low = split(direction_all)
+        rows = (((1,), (1,)), ((), ()))
+        change = (
+            lax.dot_general(basis_high, direction_high, rows, preferred_element_type=F32)
+            + lax.dot_general(basis_low, direction_high, rows, preferred_element_type=F32)
+            + lax.dot_general(basis_high, direction_low, rows, preferred_element_type=F32)
+        )
         new_weight = (weight.astype(F32) - change).astype(BF16)
         return (new_weight, new_first, new_second, new_basis)
 

time: 238 us -> 218 us (0.916)
  waiting for transfers between devices: 131 us -> 107 us
  matrix products: 37.2 us -> 39.6 us
    ppermute x24, waiting for transfers between devices: 131 us -> 107 us  [swap(): return lax.ppermute(x, axis, [(k, k ^ 1 << bit) for k in range(n)])]
    dot_general x14 -> x13, matrix products: 17.3 us -> 8.46 us  [matmul(): return jnp.dot(left, right, precision=HIGHEST)]
    dot_general x0 -> x3, matrix products: none -> 8.75 us  [the longest x1 6.17 us: shards(): lax.dot_general(basis_high, direction_low, rows, preferred_element_type=F32)]
    unnamed x26 -> x32, local copies, waits for them, and re-layouts: 19.4 us -> 18.9 us
  transfers between devices with their start and end apart: 24 -> 24, of which waited for: 20 -> 18; matrix products, arithmetic and copies ran while one was open for 11% -> 17% of each run, Pallas kernels for 0% -> 0%
where the time goes in v2:
time: 218 us
  waiting for transfers between devices  107 us (49%)
  matrix products  39.6 us (18%)
  local copies, waits for them, and re-layouts  30.9 us (14%)
  starting transfers between devices  27.6 us (13%)
  other arithmetic  10.9 us (5%)
    ppermute x24, waiting for transfers between devices, swap(): return lax.ppermute(x, axis, [(k, k ^ 1 << bit) for k in range(n)])  107 us
    ppermute x24, starting transfers between devices, swap(): return lax.ppermute(x, axis, [(k, k ^ 1 << bit) for k in range(n)])  27.6 us
    unnamed x32, local copies, waits for them, and re-layouts  18.9 us
    dot_general x6, matrix products, one(): return lax.dot_general(a, b, (dims, ((), ())), preferred_element_type=F32)  14.5 us
    dot_general x13, matrix products, matmul(): return jnp.dot(left, right, precision=HIGHEST)  8.46 us
    dot_general x1, matrix products, shards(): lax.dot_general(basis_high, direction_low, rows, preferred_element_type=F32)  6.17 us
    another operation x25, other arithmetic, all_gather(): x = jnp.stack([low, high], axis=dim + present.index(bit))  5.27 us
    dynamic_slice x3, local copies, waits for them, and re-layouts, reduce_scatter(): keep = lax.dynamic_index_in_dim(x, mine, axis=pos, keepdims=False)  4.5 us
  transfers between devices with their start and end apart: 24, of which 18 were waited for; matrix products, arithmetic and copies ran while one was open for 17% of the time, Pallas kernels for 0%

profile of v2, /device:TPU:0, one launch (start us, length us, event | category | flops | bytes accessed | tf_op | source)
XLA Modules:
  0.0 217.8 jit_solution(11615068763315327120)
XLA Ops:
  0.7 3.9 %fusion.98 = f32[2048,256]{1,0:T(8,128)S(1)} fusion(bf16[2048,1024]{1,0:T(8,128)(2,1)} %param.6, f32[1024,256]{1,0:T(8,128)} %param.9), kind=kOutput, calls=%fused_computation.183 | convolution fusion | flops 1074003968 | bytes 7340032 | tf_op jit(solution)/shard_map/dot_general | solution.py:93
  4.7 1.3 fusion.3
  6.1 3.1 %collective-permute-start = (bf16[1024,256]{1,0:T(8,128)(2,1)S(1)}, bf16[1024,256]{1,0:T(8,128)(2,1)S(1)}, u32[]{:S(2)}, u32[]{:S(2)}) collective-permute-start(bf16[1024,256]{1,0:T(8,128)(2,1)S(1)} %dynamic-slice_bitcast_fusion.2), channel_id=1, source_target_pairs={{0,1},{1,0},{2,3},{3,2},{4,5},{5,4},{6,7},{7,6},{8,9},{9,8},{10,11... | collective-permute-start | bytes 1572872 | tf_op jit(solution)/shard_map/ppermute | solution.py:45
  9.2 11.9 %collective-permute-done = bf16[1024,256]{1,0:T(8,128)(2,1)S(1)} collective-permute-done((bf16[1024,256]{1,0:T(8,128)(2,1)S(1)}, bf16[1024,256]{1,0:T(8,128)(2,1)S(1)}, u32[]{:S(2)}, u32[]{:S(2)}) %collective-permute-start) | collective-permute-done | bytes 524320 | tf_op jit(solution)/shard_map/ppermute | solution.py:45
  21.9 3.5 %fusion.11 = f32[256,2048]{1,0:T(8,128)S(1)} fusion(bf16[1024,2048]{1,0:T(8,128)(2,1)} %param.7, bf16[1024,256]{1,0:T(8,128)(2,1)S(1)} %collective-permute-done, bf16[2,1024,256]{2,1,0:T(8,128)(2,1)S(1)} %bitcast.177, s32[]{:T(128)S(6)} %select_n.212), kind=kOutput, calls=%fused_computation.42 | convolution fusion | flops 1074790400 | bytes 7340036 | tf_op jit(solution)/shard_map/dot_general | solution.py:29
  25.4 2.5 %convolution_add_fusion = f32[256,2048]{1,0:T(8,128)S(1)} fusion(f32[256,2048]{1,0:T(8,128)S(1)} %fusion.11, bf16[1024,2048]{1,0:T(8,128)(2,1)S(1)} %copy-done.3, bf16[1024,256]{1,0:T(8,128)(2,1)} %copy-done.9, bf16[2,1024,256]{2,1,0:T(8,128)(2,1)} %bitcast.178, s32[]{:T(128)S(6)} %select_n.212), kind=kOutput, calls=%fused_computation.6 | convolution fusion | flops 1074528256 | bytes 9437188 | tf_op jit(solution)/shard_map/dot_general | solution.py:29
  27.9 3.0 %reshape.30 = f32[256,2,2,2,2,128]{5,4,3,2,1,0:T(2,128)} reshape(f32[256,2048]{1,0:T(8,128)S(1)} %convolution_add_fusion) | data formatting | bytes 4194304 | tf_op jit(solution)/shard_map/reshape | solution.py:53
  30.9 4.4 %constant_dynamic-slice_fusion.3 = (f32[256,2,2,2,1,128]{5,4,3,2,1,0:T(1,128)S(1)}, f32[256,2,2,2,1,128]{5,4,3,2,1,0:T(1,128)S(1)}) fusion(f32[256,2,2,2,2,128]{5,4,3,2,1,0:T(2,128)} %reshape.30, s32[]{:T(128)S(6)} %select_n.214, s32[]{:T(128)S(6)} %select_n.215), kind=kLoop, calls=%fused_computation.141 | loop fusion | bytes 4194312 | tf_op jit(solution)/shard_map/jit(dynamic_index_in_dim)/dynamic_slice | solution.py:58
  35.2 1.2 copy.64
  36.4 2.9 %collective-permute-done.1 = f32[256,2,2,2,128]{4,0,3,2,1:T(8,128)S(1)} collective-permute-done((f32[256,2,2,2,128]{4,0,3,2,1:T(8,128)}, f32[256,2,2,2,128]{4,0,3,2,1:T(8,128)S(1)}, u32[]{:S(2)}, u32[]{:S(2)}) %collective-permute-start.1) | collective-permute-done | bytes 1048608 | tf_op jit(solution)/shard_map/ppermute | solution.py:45
  39.3 1.0 copy-done.7
  40.2 1.5 bitcast_add_fusion.2
  41.8 1.8 collective-permute-start.2
  43.6 12.3 %collective-permute-done.2 = f32[256,2,2,128]{3,0,2,1:T(8,128)S(1)} collective-permute-done((f32[256,2,2,128]{3,0,2,1:T(8,128)S(1)}, f32[256,2,2,128]{3,0,2,1:T(8,128)S(1)}, u32[]{:S(2)}, u32[]{:S(2)}) %collective-permute-start.2) | collective-permute-done | bytes 524320 | tf_op jit(solution)/shard_map/ppermute | solution.py:45
  55.9 1.9 collective-permute-start.3
  57.8 5.8 %collective-permute-done.3 = f32[256,2,128]{2,0,1:T(8,128)S(1)} collective-permute-done((f32[256,2,128]{2,0,1:T(8,128)S(1)}, f32[256,2,128]{2,0,1:T(8,128)S(1)}, u32[]{:S(2)}, u32[]{:S(2)}) %collective-permute-start.3) | collective-permute-done | bytes 262176 | tf_op jit(solution)/shard_map/ppermute | solution.py:45
  63.7 2.8 %collective-permute-start.4 = (f32[256,128]{0,1:T(8,128)S(1)}, f32[256,128]{0,1:T(8,128)S(1)}, u32[]{:S(2)}, u32[]{:S(2)}) collective-permute-start(f32[256,128]{0,1:T(8,128)S(1)} %bitcast.181), channel_id=1, source_target_pairs={{0,16},{2,18},{4,20},{6,22},{8,24},{10,26},{12,28},{14,30},{16,0},... | collective-permute-start | bytes 393224 | tf_op jit(solution)/shard_map/ppermute | solution.py:45
  66.6 4.8 %collective-permute-done.4 = f32[256,128]{0,1:T(8,128)S(1)} collective-permute-done((f32[256,128]{0,1:T(8,128)S(1)}, f32[256,128]{0,1:T(8,128)S(1)}, u32[]{:S(2)}, u32[]{:S(2)}) %collective-permute-start.4) | collective-permute-done | bytes 131104 | tf_op jit(solution)/shard_map/ppermute | solution.py:45
  71.4 1.6 collective-permute-start.5
  73.3 3.2 %collective-permute-done.5 = f32[256,128]{0,1:T(8,128)S(1)} collective-permute-done((f32[256,128]{0,1:T(8,128)S(1)}, f32[256,128]{0,1:T(8,128)S(1)}, u32[]{:S(2)}, u32[]{:S(2)}) %collective-permute-start.5) | collective-permute-done | bytes 131104 | tf_op jit(solution)/shard_map/ppermute | solution.py:45
  77.2 1.1 collective-permute-start.10
  78.3 6.3 %collective-permute-done.10 = f32[256,128]{0,1:T(8,128)S(1)} collective-permute-done((f32[256,128]{0,1:T(8,128)S(1)}, f32[256,128]{0,1:T(8,128)S(1)}, u32[]{:S(2)}, u32[]{:S(2)}) %collective-permute-start.10) | collective-permute-done | bytes 131104 | tf_op jit(solution)/shard_map/ppermute | solution.py:45
  84.7 6.4 %collective-permute-done.11 = f32[256,2,128]{0,2,1:T(8,128)S(1)} collective-permute-done((f32[256,2,128]{0,2,1:T(8,128)S(1)}, f32[256,2,128]{0,2,1:T(8,128)S(1)}, u32[]{:S(2)}, u32[]{:S(2)}) %collective-permute-start.11) | collective-permute-done | bytes 262176 | tf_op jit(solution)/shard_map/ppermute | solution.py:45
  91.1 1.6 collective-permute-start.12
  92.8 7.6 %collective-permute-done.12 = f32[256,2,2,128]{0,3,1,2:T(8,128)S(1)} collective-permute-done((f32[256,2,2,128]{0,3,1,2:T(8,128)S(1)}, f32[256,2,2,128]{0,3,1,2:T(8,128)S(1)}, u32[]{:S(2)}, u32[]{:S(2)}) %collective-permute-start.12) | collective-permute-done | bytes 524320 | tf_op jit(solution)/shard_map/ppermute | solution.py:45
  100.5 1.1 pad_maximum_fusion.3
  101.6 2.9 %collective-permute-done.13 = f32[256,2,2,2,128]{0,4,1,2,3:T(8,128)S(1)} collective-permute-done((f32[256,2,2,2,128]{0,4,1,2,3:T(8,128)}, f32[256,2,2,2,128]{0,4,1,2,3:T(8,128)S(1)}, u32[]{:S(2)}, u32[]{:S(2)}) %collective-permute-start.13) | collective-permute-done | bytes 1048608 | tf_op jit(solution)/shard_map/ppermute | solution.py:45
  105.2 1.7 copy-done.4
  107.0 1.3 fusion.101
  108.3 1.3 fusion.8
  109.6 1.6 collective-permute-start.14
  111.2 1.2 collective-permute-start.6
  112.4 7.8 %collective-permute-done.6 = f32[128,256]{1,0:T(8,128)S(1)} collective-permute-done((f32[128,256]{1,0:T(8,128)S(1)}, f32[128,256]{1,0:T(8,128)S(1)}, u32[]{:S(2)}, u32[]{:S(2)}) %collective-permute-start.6) | collective-permute-done | bytes 131104 | tf_op jit(solution)/shard_map/ppermute | solution.py:45
  121.0 2.7 %collective-permute-done.14 = bf16[1024,256]{0,1:T(8,128)(2,1)S(1)} collective-permute-done((bf16[1024,256]{0,1:T(8,128)(2,1)S(1)}, bf16[1024,256]{0,1:T(8,128)(2,1)S(1)}, u32[]{:S(2)}, u32[]{:S(2)}) %collective-permute-start.14) | collective-permute-done | bytes 524320 | tf_op jit(solution)/shard_map/ppermute | solution.py:45
  124.6 3.6 %fusion.102 = f32[256,1024]{1,0:T(8,128)S(1)} fusion(bf16[2048,256]{1,0:T(8,128)(2,1)S(1)} %bitcast.179, bf16[2048,1024]{1,0:T(8,128)(2,1)} %param.6), kind=kOutput, calls=%fused_computation.186 | convolution fusion | flops 1073741824 | bytes 6291456 | tf_op jit(solution)/shard_map/dot_general | solution.py:29
  128.2 2.3 %fusion.6 = f32[1024,256]{0,1:T(8,128)} fusion(f32[256,1024]{1,0:T(8,128)S(1)} %fusion.102, bf16[2048,1024]{1,0:T(8,128)(2,1)S(1)} %copy-done.2, bf16[2048,256]{1,0:T(8,128)(2,1)S(1)} %bitcast.180), kind=kOutput, calls=%fused_computation.18 | convolution fusion | flops 1075576832 | bytes 7340032 | tf_op jit(solution)/shard_map/dot_general | solution.py:29
  130.5 1.6 copy.52
  132.2 1.0 select_bitcast_fusion.17
  133.3 1.6 collective-permute-start.8
  135.0 0.8 collective-permute-start.16
  135.8 12.3 %collective-permute-done.8 = f32[2,2,128,256]{3,2,1,0:T(8,128)S(1)} collective-permute-done((f32[2,2,128,256]{3,2,1,0:T(8,128)S(1)}, f32[2,2,128,256]{3,2,1,0:T(8,128)S(1)}, u32[]{:S(2)}, u32[]{:S(2)}) %collective-permute-start.8) | collective-permute-done | bytes 524320 | tf_op jit(solution)/shard_map/ppermute | solution.py:45
  148.2 1.1 pad_maximum_fusion.2
  149.3 3.9 %collective-permute-done.16 = f32[2,2,64,256]{3,2,1,0:T(8,128)S(1)} collective-permute-done((f32[2,2,64,256]{3,2,1,0:T(8,128)S(1)}, f32[2,2,64,256]{3,2,1,0:T(8,128)S(1)}, u32[]{:S(2)}, u32[]{:S(2)}) %collective-permute-start.16) | collective-permute-done | bytes 262176 | tf_op jit(solution)/shard_map/ppermute | solution.py:45
  153.4 5.0 %collective-permute-done.17 = f32[2,64,256]{2,1,0:T(8,128)S(1)} collective-permute-done((f32[2,64,256]{2,1,0:T(8,128)S(1)}, f32[2,64,256]{2,1,0:T(8,128)S(1)}, u32[]{:S(2)}, u32[]{:S(2)}) %collective-permute-start.17) | collective-permute-done | bytes 131104 | tf_op jit(solution)/shard_map/ppermute | solution.py:45
  159.1 1.6 collective-permute-start.18
  160.7 6.4 %copy.38 = bf16[1024,2048]{0,1:T(8,128)(2,1)} copy(bf16[1024,2048]{1,0:T(8,128)(2,1)} %param.8) | data formatting | bytes 8388608 | tf_op args[2]
  168.6 0.8 bitcast_add_fusion.12
  169.5 1.3 collective-permute-start.19
  171.0 3.7 %collective-permute-done.19 = f32[64,256]{1,0:T(8,128)S(1)} collective-permute-done((f32[64,256]{1,0:T(8,128)S(1)}, f32[64,256]{1,0:T(8,128)S(1)}, u32[]{:S(2)}, u32[]{:S(2)}) %collective-permute-start.19) | collective-permute-done | bytes 65568 | tf_op jit(solution)/shard_map/ppermute | solution.py:45
  174.7 2.2 %collective-permute-start.20 = (f32[2,64,256]{2,1,0:T(8,128)S(1)}, f32[2,64,256]{2,1,0:T(8,128)S(1)}, u32[]{:S(2)}, u32[]{:S(2)}) collective-permute-start(f32[2,64,256]{2,1,0:T(8,128)S(1)} %pad_maximum_fusion.13), channel_id=1, source_target_pairs={{0,8},{2,10},{4,12},{6,14},{8,0},{10,2},{12,4},{14,6},{16,24},{18,... | collective-permute-start | bytes 393224 | tf_op jit(solution)/shard_map/ppermute | solution.py:45
  177.1 2.8 %collective-permute-done.20 = f32[2,64,256]{2,1,0:T(8,128)S(1)} collective-permute-done((f32[2,64,256]{2,1,0:T(8,128)S(1)}, f32[2,64,256]{2,1,0:T(8,128)S(1)}, u32[]{:S(2)}, u32[]{:S(2)}) %collective-permute-start.20) | collective-permute-done | bytes 131104 | tf_op jit(solution)/shard_map/ppermute | solution.py:45
  180.0 1.5 collective-permute-start.21
  181.7 4.6 %collective-permute-done.21 = f32[2,2,64,256]{3,2,1,0:T(8,128)S(1)} collective-permute-done((f32[2,2,64,256]{3,2,1,0:T(8,128)S(1)}, f32[2,2,64,256]{3,2,1,0:T(8,128)S(1)}, u32[]{:S(2)}, u32[]{:S(2)}) %collective-permute-start.21) | collective-permute-done | bytes 262176 | tf_op jit(solution)/shard_map/ppermute | solution.py:45
  186.6 1.3 fusion.92
  187.9 1.3 fusion.95
  190.1 2.6 %convolution_bitcast_fusion.1 = f32[256,256]{1,0:T(8,128)} fusion(f32[2,2,2,1,64,256]{5,4,3,2,1,0:T(8,128)S(1)} %get-tuple-element.33, f32[2,2,2,1,64,256]{5,4,3,2,1,0:T(8,128)S(1)} %get-tuple-element.32), kind=kOutput, calls=%fused_computation.24 | convolution fusion | flops 805568512 | bytes 1310720 | tf_op jit(solution)/shard_map/dot_general | solution.py:120
  192.7 1.5 collective-permute-start.23
  194.2 6.2 %fusion.1 = bf16[1024,2048]{0,1:T(8,128)(2,1)} fusion(f32[1024,2048]{0,1:T(8,128)S(1)} %fusion.92, f32[2048,1024]{1,0:T(8,128)S(1)} %fusion.95, bf16[1024,2048]{0,1:T(8,128)(2,1)} %copy.38, bf16[2048,256]{1,0:T(8,128)(2,1)S(1)} %get-tuple-element.20, f32[1024,256]{1,0:T(8,128)S(1)} %copy-done), kind=kOutput, calls=%fused_computation.2 | convolution fusion | flops 1084489728 | bytes 27262976 | tf_op jit(solution)/shard_map/dot_general | solution.py:138
  200.3 6.4 %copy.56 = bf16[1024,2048]{1,0:T(8,128)(2,1)} copy(bf16[1024,2048]{0,1:T(8,128)(2,1)} %fusion.1) | data formatting | bytes 8388608
  206.8 1.7 select_reduce_fusion
  209.1 1.0 fusion.16
  210.1 1.0 fusion.15
  211.0 1.0 fusion.14
  215.8 2.0 fusion.104
  (95 shorter events, 13.0 us)
Async XLA Ops:
  0.6 4.0 %copy-start.1 = (bf16[2048,1024]{1,0:T(8,128)(2,1)S(1)}, bf16[2048,1024]{1,0:T(8,128)(2,1)}, u32[]{:S(2)}) copy-start(bf16[2048,1024]{1,0:T(8,128)(2,1)} %param.6) | copy-start | bytes 12582916
  0.6 4.0 %copy-start = (f32[1024,256]{1,0:T(8,128)S(1)}, f32[1024,256]{1,0:T(8,128)}, u32[]{:S(2)}) copy-start(f32[1024,256]{1,0:T(8,128)} %param.9) | copy-start | bytes 3145732
  6.0 15.1 %copy-start.8 = (bf16[2048,256]{1,0:T(8,128)(2,1)}, bf16[2048,256]{1,0:T(8,128)(2,1)S(1)}, u32[]{:S(2)}) copy-start(bf16[2048,256]{1,0:T(8,128)(2,1)S(1)} %fusion.3) | copy-start | bytes 3145732
  6.1 15.0 %collective-permute-start = (bf16[1024,256]{1,0:T(8,128)(2,1)S(1)}, bf16[1024,256]{1,0:T(8,128)(2,1)S(1)}, u32[]{:S(2)}, u32[]{:S(2)}) collective-permute-start(bf16[1024,256]{1,0:T(8,128)(2,1)S(1)} %dynamic-slice_bitcast_fusion.2), channel_id=1, source_target_pairs={{0,1},{1,0},{2,3},{3,2},{4,5},{5,4},{6,7},{7,6},{8,9},{9,8},{10,11... | collective-permute-start | bytes 1572872 | tf_op jit(solution)/shard_map/ppermute | solution.py:45
  9.2 16.2 %copy-start.3 = (bf16[1024,2048]{1,0:T(8,128)(2,1)S(1)}, bf16[1024,2048]{1,0:T(8,128)(2,1)}, u32[]{:S(2)}) copy-start(bf16[1024,2048]{1,0:T(8,128)(2,1)} %param.7) | copy-start | bytes 12582916
  21.1 0.8 copy-start.9
  36.4 2.9 %collective-permute-start.1 = (f32[256,2,2,2,128]{4,0,3,2,1:T(8,128)}, f32[256,2,2,2,128]{4,0,3,2,1:T(8,128)S(1)}, u32[]{:S(2)}, u32[]{:S(2)}) collective-permute-start(f32[256,2,2,2,128]{4,0,3,2,1:T(8,128)} %bitcast.172), channel_id=1, source_target_pairs={{0,2},{2,0},{4,6},{6,4},{8,10},{10,8},{12,14},{14,12},{16,18},{18,... | collective-permute-start | bytes 3145736 | tf_op jit(solution)/shard_map/ppermute | solution.py:45
  39.3 1.0 copy-start.7
  40.2 32.8 %copy-start.11 = (f32[256,128]{1,0:T(8,128)S(1)}, f32[256,128]{1,0:T(8,128)}, u32[]{:S(2)}) copy-start(f32[256,128]{1,0:T(8,128)} %param.10) | copy-start | bytes 393220
  40.2 32.9 %copy-start.12 = (f32[256,128]{1,0:T(8,128)S(1)}, f32[256,128]{1,0:T(8,128)}, u32[]{:S(2)}) copy-start(f32[256,128]{1,0:T(8,128)} %param.11) | copy-start | bytes 393220
  41.8 14.0 %collective-permute-start.2 = (f32[256,2,2,128]{3,0,2,1:T(8,128)S(1)}, f32[256,2,2,128]{3,0,2,1:T(8,128)S(1)}, u32[]{:S(2)}, u32[]{:S(2)}) collective-permute-start(f32[256,2,2,128]{3,0,2,1:T(8,128)S(1)} %dynamic-slice_bitcast_fusion.1), channel_id=1, source_target_pairs={{0,4},{2,6},{4,0},{6,2},{8,12},{10,14},{12,8},{14,10},{16,20},{18,... | collective-permute-start | bytes 1572872 | tf_op jit(solution)/shard_map/ppermute | solution.py:45
  55.9 7.6 %collective-permute-start.3 = (f32[256,2,128]{2,0,1:T(8,128)S(1)}, f32[256,2,128]{2,0,1:T(8,128)S(1)}, u32[]{:S(2)}, u32[]{:S(2)}) collective-permute-start(f32[256,2,128]{2,0,1:T(8,128)S(1)} %dynamic-slice_bitcast_fusion.4), channel_id=1, source_target_pairs={{0,8},{2,10},{4,12},{6,14},{8,0},{10,2},{12,4},{14,6},{16,24},{18,... | collective-permute-start | bytes 786440 | tf_op jit(solution)/shard_map/ppermute | solution.py:45
  63.7 7.7 %collective-permute-start.4 = (f32[256,128]{0,1:T(8,128)S(1)}, f32[256,128]{0,1:T(8,128)S(1)}, u32[]{:S(2)}, u32[]{:S(2)}) collective-permute-start(f32[256,128]{0,1:T(8,128)S(1)} %bitcast.181), channel_id=1, source_target_pairs={{0,16},{2,18},{4,20},{6,22},{8,24},{10,26},{12,28},{14,30},{16,0},... | collective-permute-start | bytes 393224 | tf_op jit(solution)/shard_map/ppermute | solution.py:45
  71.4 5.0 %collective-permute-start.5 = (f32[256,128]{0,1:T(8,128)S(1)}, f32[256,128]{0,1:T(8,128)S(1)}, u32[]{:S(2)}, u32[]{:S(2)}) collective-permute-start(f32[256,128]{0,1:T(8,128)S(1)} %bitcast_add_fusion.11), channel_id=1, source_target_pairs={{0,1},{1,0},{2,3},{3,2},{4,5},{5,4},{6,7},{7,6},{8,9},{9,8},{10,11... | collective-permute-start | bytes 393224 | tf_op jit(solution)/shard_map/ppermute | solution.py:45
  77.2 7.4 %collective-permute-start.10 = (f32[256,128]{0,1:T(8,128)S(1)}, f32[256,128]{0,1:T(8,128)S(1)}, u32[]{:S(2)}, u32[]{:S(2)}) collective-permute-start(f32[256,128]{0,1:T(8,128)S(1)} %get-tuple-element.25), channel_id=1, source_target_pairs={{0,16},{2,18},{4,20},{6,22},{8,24},{10,26},{12,28},{14,30},{16,0},... | collective-permute-start | bytes 393224 | tf_op jit(solution)/shard_map/ppermute | solution.py:45
  84.6 6.4 %collective-permute-start.11 = (f32[256,2,128]{0,2,1:T(8,128)S(1)}, f32[256,2,128]{0,2,1:T(8,128)S(1)}, u32[]{:S(2)}, u32[]{:S(2)}) collective-permute-start(f32[256,2,128]{0,2,1:T(8,128)S(1)} %pad_maximum_fusion.11), channel_id=1, source_target_pairs={{0,8},{2,10},{4,12},{6,14},{8,0},{10,2},{12,4},{14,6},{16,24},{18,... | collective-permute-start | bytes 786440 | tf_op jit(solution)/shard_map/ppermute | solution.py:45
  91.1 9.2 %collective-permute-start.12 = (f32[256,2,2,128]{0,3,1,2:T(8,128)S(1)}, f32[256,2,2,128]{0,3,1,2:T(8,128)S(1)}, u32[]{:S(2)}, u32[]{:S(2)}) collective-permute-start(f32[256,2,2,128]{0,3,1,2:T(8,128)S(1)} %pad_maximum_fusion.8), channel_id=1, source_target_pairs={{0,4},{2,6},{4,0},{6,2},{8,12},{10,14},{12,8},{14,10},{16,20},{18,... | collective-permute-start | bytes 1572872 | tf_op jit(solution)/shard_map/ppermute | solution.py:45
  101.6 2.9 %collective-permute-start.13 = (f32[256,2,2,2,128]{0,4,1,2,3:T(8,128)}, f32[256,2,2,2,128]{0,4,1,2,3:T(8,128)S(1)}, u32[]{:S(2)}, u32[]{:S(2)}) collective-permute-start(f32[256,2,2,2,128]{0,4,1,2,3:T(8,128)} %pad_maximum_fusion.3), channel_id=1, source_target_pairs={{0,2},{2,0},{4,6},{6,4},{8,10},{10,8},{12,14},{14,12},{16,18},{18,... | collective-permute-start | bytes 3145736 | tf_op jit(solution)/shard_map/ppermute | solution.py:45
  104.8 2.2 %copy-start.4 = (bf16[1024,2048]{1,0:T(8,128)(2,1)S(1)}, bf16[1024,2048]{1,0:T(8,128)(2,1)}, u32[]{:S(2)}) copy-start(bf16[1024,2048]{1,0:T(8,128)(2,1)} %param.7) | copy-start | bytes 12582916
  109.6 14.0 %collective-permute-start.14 = (bf16[1024,256]{0,1:T(8,128)(2,1)S(1)}, bf16[1024,256]{0,1:T(8,128)(2,1)S(1)}, u32[]{:S(2)}, u32[]{:S(2)}) collective-permute-start(bf16[1024,256]{0,1:T(8,128)(2,1)S(1)} %fusion.8), channel_id=1, source_target_pairs={{0,1},{1,0},{2,3},{3,2},{4,5},{5,4},{6,7},{7,6},{8,9},{9,8},{10,11... | collective-permute-start | bytes 1572872 | tf_op jit(solution)/shard_map/ppermute | solution.py:45
  111.2 9.0 %collective-permute-start.6 = (f32[128,256]{1,0:T(8,128)S(1)}, f32[128,256]{1,0:T(8,128)S(1)}, u32[]{:S(2)}, u32[]{:S(2)}) collective-permute-start(f32[128,256]{1,0:T(8,128)S(1)} %get-tuple-element.22), channel_id=1, source_target_pairs={{0,16},{2,18},{4,20},{6,22},{8,24},{10,26},{12,28},{14,30},{16,0},... | collective-permute-start | bytes 393224 | tf_op jit(solution)/shard_map/ppermute | solution.py:45
  121.0 11.2 %collective-permute-start.7 = (f32[2,128,256]{2,1,0:T(8,128)}, f32[2,128,256]{2,1,0:T(8,128)}, u32[]{:S(2)}, u32[]{:S(2)}) collective-permute-start(f32[2,128,256]{2,1,0:T(8,128)} %pad_maximum_fusion.10), channel_id=1, source_target_pairs={{0,8},{2,10},{4,12},{6,14},{8,0},{10,2},{12,4},{14,6},{16,24},{18,... | collective-permute-start | bytes 786440 | tf_op jit(solution)/shard_map/ppermute | solution.py:45
  124.6 3.6 %copy-start.2 = (bf16[2048,1024]{1,0:T(8,128)(2,1)S(1)}, bf16[2048,1024]{1,0:T(8,128)(2,1)}, u32[]{:S(2)}) copy-start(bf16[2048,1024]{1,0:T(8,128)(2,1)} %param.6) | copy-start | bytes 12582916
  132.1 2.7 %collective-permute-start.15 = (f32[2,2,2,64,256]{4,3,2,1,0:T(8,128)S(1)}, f32[2,2,2,64,256]{4,3,2,1,0:T(8,128)S(1)}, u32[]{:S(2)}, u32[]{:S(2)}) collective-permute-start(f32[2,2,2,64,256]{4,3,2,1,0:T(8,128)S(1)} %dynamic-slice_bitcast_fusion), channel_id=1, source_target_pairs={{0,2},{2,0},{4,6},{6,4},{8,10},{10,8},{12,14},{14,12},{16,18},{18,... | collective-permute-start | bytes 1572872 | tf_op jit(solution)/shard_map/ppermute | solution.py:45
  133.3 14.9 %collective-permute-start.8 = (f32[2,2,128,256]{3,2,1,0:T(8,128)S(1)}, f32[2,2,128,256]{3,2,1,0:T(8,128)S(1)}, u32[]{:S(2)}, u32[]{:S(2)}) collective-permute-start(f32[2,2,128,256]{3,2,1,0:T(8,128)S(1)} %pad_maximum_fusion.7), channel_id=1, source_target_pairs={{0,4},{2,6},{4,0},{6,2},{8,12},{10,14},{12,8},{14,10},{16,20},{18,... | collective-permute-start | bytes 1572872 | tf_op jit(solution)/shard_map/ppermute | solution.py:45
  135.0 18.3 %collective-permute-start.16 = (f32[2,2,64,256]{3,2,1,0:T(8,128)S(1)}, f32[2,2,64,256]{3,2,1,0:T(8,128)S(1)}, u32[]{:S(2)}, u32[]{:S(2)}) collective-permute-start(f32[2,2,64,256]{3,2,1,0:T(8,128)S(1)} %dynamic-slice_bitcast_fusion.3), channel_id=1, source_target_pairs={{0,4},{2,6},{4,0},{6,2},{8,12},{10,14},{12,8},{14,10},{16,20},{18,... | collective-permute-start | bytes 786440 | tf_op jit(solution)/shard_map/ppermute | solution.py:45
  149.3 21.5 %collective-permute-start.9 = (f32[2,2,2,128,256]{4,3,2,1,0:T(8,128)}, f32[2,2,2,128,256]{4,3,2,1,0:T(8,128)S(1)}, u32[]{:S(2)}, u32[]{:S(2)}) collective-permute-start(f32[2,2,2,128,256]{4,3,2,1,0:T(8,128)} %pad_maximum_fusion.2), channel_id=1, source_target_pairs={{0,2},{2,0},{4,6},{6,4},{8,10},{10,8},{12,14},{14,12},{16,18},{18,... | collective-permute-start | bytes 3145736 | tf_op jit(solution)/shard_map/ppermute | solution.py:45
  153.3 5.1 %collective-permute-start.17 = (f32[2,64,256]{2,1,0:T(8,128)S(1)}, f32[2,64,256]{2,1,0:T(8,128)S(1)}, u32[]{:S(2)}, u32[]{:S(2)}) collective-permute-start(f32[2,64,256]{2,1,0:T(8,128)S(1)} %dynamic-slice_bitcast_fusion.5), channel_id=1, source_target_pairs={{0,8},{2,10},{4,12},{6,14},{8,0},{10,2},{12,4},{14,6},{16,24},{18,... | collective-permute-start | bytes 393224 | tf_op jit(solution)/shard_map/ppermute | solution.py:45
  159.1 8.0 %copy-start.10 = (f32[256,128]{0,1:T(8,128)S(1)}, f32[256,128]{0,1:T(8,128)}, u32[]{:S(2)}) copy-start(f32[256,128]{0,1:T(8,128)} %get-tuple-element.23) | copy-start | bytes 393220
  159.1 9.6 %collective-permute-start.18 = (f32[64,256]{1,0:T(8,128)}, f32[64,256]{1,0:T(8,128)}, u32[]{:S(2)}, u32[]{:S(2)}) collective-permute-start(f32[64,256]{1,0:T(8,128)} %dynamic-slice_bitcast_fusion.6), channel_id=1, source_target_pairs={{0,16},{2,18},{4,20},{6,22},{8,24},{10,26},{12,28},{14,30},{16,0},... | collective-permute-start | bytes 196616 | tf_op jit(solution)/shard_map/ppermute | solution.py:45
  169.5 5.2 %collective-permute-start.19 = (f32[64,256]{1,0:T(8,128)S(1)}, f32[64,256]{1,0:T(8,128)S(1)}, u32[]{:S(2)}, u32[]{:S(2)}) collective-permute-start(f32[64,256]{1,0:T(8,128)S(1)} %bitcast_add_fusion.12), channel_id=1, source_target_pairs={{0,16},{2,18},{4,20},{6,22},{8,24},{10,26},{12,28},{14,30},{16,0},... | collective-permute-start | bytes 196616 | tf_op jit(solution)/shard_map/ppermute | solution.py:45
  174.7 5.2 %collective-permute-start.20 = (f32[2,64,256]{2,1,0:T(8,128)S(1)}, f32[2,64,256]{2,1,0:T(8,128)S(1)}, u32[]{:S(2)}, u32[]{:S(2)}) collective-permute-start(f32[2,64,256]{2,1,0:T(8,128)S(1)} %pad_maximum_fusion.13), channel_id=1, source_target_pairs={{0,8},{2,10},{4,12},{6,14},{8,0},{10,2},{12,4},{14,6},{16,24},{18,... | collective-permute-start | bytes 393224 | tf_op jit(solution)/shard_map/ppermute | solution.py:45
  180.0 6.4 %collective-permute-start.21 = (f32[2,2,64,256]{3,2,1,0:T(8,128)S(1)}, f32[2,2,64,256]{3,2,1,0:T(8,128)S(1)}, u32[]{:S(2)}, u32[]{:S(2)}) collective-permute-start(f32[2,2,64,256]{3,2,1,0:T(8,128)S(1)} %pad_maximum_fusion.12), channel_id=1, source_target_pairs={{0,4},{2,6},{4,0},{6,2},{8,12},{10,14},{12,8},{14,10},{16,20},{18,... | collective-permute-start | bytes 786440 | tf_op jit(solution)/shard_map/ppermute | solution.py:45
  186.5 2.7 %collective-permute-start.22 = (f32[2,2,2,64,256]{4,3,2,1,0:T(8,128)S(1)}, f32[2,2,2,64,256]{4,3,2,1,0:T(8,128)S(1)}, u32[]{:S(2)}, u32[]{:S(2)}) collective-permute-start(f32[2,2,2,64,256]{4,3,2,1,0:T(8,128)S(1)} %pad_maximum_fusion.9), channel_id=1, source_target_pairs={{0,2},{2,0},{4,6},{6,4},{8,10},{10,8},{12,14},{14,12},{16,18},{18,... | collective-permute-start | bytes 1572872 | tf_op jit(solution)/shard_map/ppermute | solution.py:45
  189.3 0.8 copy-start.5
  192.7 14.1 %collective-permute-start.23 = (f32[256,256]{1,0:T(8,128)}, f32[256,256]{1,0:T(8,128)}, u32[]{:S(2)}, u32[]{:S(2)}) collective-permute-start(f32[256,256]{1,0:T(8,128)} %convolution_bitcast_fusion.1), channel_id=1, source_target_pairs={{0,1},{1,0},{2,3},{3,2},{4,5},{5,4},{6,7},{7,6},{8,9},{9,8},{10,11... | collective-permute-start | bytes 786440 | tf_op jit(solution)/shard_map/ppermute | solution.py:45
  206.7 5.7 %copy-start.6 = (f32[2,2,2,1,64,256]{5,4,3,2,1,0:T(8,128)S(1)}, f32[2,2,2,1,64,256]{5,4,3,2,1,0:T(8,128)}, u32[]{:S(2)}) copy-start(f32[2,2,2,1,64,256]{5,4,3,2,1,0:T(8,128)} %copy-done.5) | copy-start | bytes 1572868

commit v3 on v2

--- a/solution.py
+++ b/solution.py
@@ -96,9 +96,10 @@
         tokens_basis = reduce_scatter(
             tokens_basis.astype(BF16), "group", group_count, 0, group_up
         ).astype(F32)
-        projected_part = dot_mixed(tokens_basis, grad_out, ((0,), (0,)))
-        projected = reduce_scatter(projected_part, "dp", dp_count, 1, dp_up)
-        projected = all_reduce(projected, "group", group_count)
+        projected_part = dot_mixed(grad_out, tokens_basis, ((0,), (0,)))
+        projected_rows = reduce_scatter(projected_part, "dp", dp_count, 0, dp_up)
+        projected_rows = all_reduce(projected_rows, "group", group_count)
+        projected = projected_rows.T
 
         new_first = BETA_ONE * first_moment + (1.0 - BETA_ONE) * projected
         new_second = BETA_TWO * second_moment + (1.0 - BETA_TWO) * projected * projected
@@ -108,10 +109,10 @@
             / (jnp.sqrt(new_second / (1.0 - BETA_TWO**STEP)) + ADAM_EPS)
         )
 
-        projected_all = all_gather(projected, "dp", dp_count, 1, dp_down)
+        projected_all = all_gather(projected_rows, "dp", dp_count, 0, dp_down)
         direction_all = all_gather(direction.T, "dp", dp_count, 0, dp_down)
 
-        tokens_sub = dot_mixed(grad_out, projected_all, ((1,), (1,)))
+        tokens_sub = dot_mixed(grad_out, projected_all, ((1,), (0,)))
         tokens_sub = all_gather(tokens_sub.astype(BF16), "group", group_count, 0, group_down)
         subspace_part = dot_mixed(inputs, tokens_sub, ((0,), (0,)))
         subspace = reduce_scatter(subspace_part, "dp", dp_count, 0, dp_up)

time: 218 us -> 219 us (level)
    dynamic_slice x3 -> x2, local copies, waits for them, and re-layouts: 4.5 us -> 5.69 us  [reduce_scatter(): keep = lax.dynamic_index_in_dim(x, mine, axis=pos, keepdims=False)]
    unnamed x32 -> x30, local copies, waits for them, and re-layouts: 18.9 us -> 17.9 us
where the time goes in v3:
time: 219 us; the launch traced here: 218 us
  waiting for transfers between devices  106 us (48%)
  matrix products  39.8 us (18%)
  local copies, waits for them, and re-layouts  32.3 us (15%)
  starting transfers between devices  27.6 us (13%)
  other arithmetic  10.9 us (5%)
    ppermute x24, waiting for transfers between devices, swap(): return lax.ppermute(x, axis, [(k, k ^ 1 << bit) for k in range(n)])  106 us
    ppermute x24, starting transfers between devices, swap(): return lax.ppermute(x, axis, [(k, k ^ 1 << bit) for k in range(n)])  27.6 us
    unnamed x30, local copies, waits for them, and re-layouts  17.9 us
    dot_general x6, matrix products, one(): return lax.dot_general(a, b, (dims, ((), ())), preferred_element_type=F32)  14.5 us
    dot_general x13, matrix products, matmul(): return jnp.dot(left, right, precision=HIGHEST)  8.7 us
    dot_general x1, matrix products, shards(): lax.dot_general(basis_high, direction_low, rows, preferred_element_type=F32)  6.17 us
    dynamic_slice x2, local copies, waits for them, and re-layouts, reduce_scatter(): keep = lax.dynamic_index_in_dim(x, mine, axis=pos, keepdims=False)  5.69 us
    another operation x25, other arithmetic, all_gather(): x = jnp.stack([low, high], axis=dim + present.index(bit))  5.29 us
  transfers between devices with their start and end apart: 24, of which 18 were waited for; matrix products, arithmetic and copies ran while one was open for 17% of the time, Pallas kernels for 0%

profile of v3, /device:TPU:0, one launch (start us, length us, event | category | flops | bytes accessed | tf_op | source)
XLA Modules:
  0.0 218.3 jit_solution(11755413364954005227)
XLA Ops:
  0.7 3.9 %fusion.100 = f32[2048,256]{1,0:T(8,128)S(1)} fusion(bf16[2048,1024]{1,0:T(8,128)(2,1)} %param.6, f32[1024,256]{1,0:T(8,128)} %param.9), kind=kOutput, calls=%fused_computation.183 | convolution fusion | flops 1074003968 | bytes 7340032 | tf_op jit(solution)/shard_map/dot_general | solution.py:93
  4.7 1.3 fusion.4
  6.1 3.1 %collective-permute-start = (bf16[1024,256]{1,0:T(8,128)(2,1)S(1)}, bf16[1024,256]{1,0:T(8,128)(2,1)S(1)}, u32[]{:S(2)}, u32[]{:S(2)}) collective-permute-start(bf16[1024,256]{1,0:T(8,128)(2,1)S(1)} %dynamic-slice_bitcast_fusion.2), channel_id=1, source_target_pairs={{0,1},{1,0},{2,3},{3,2},{4,5},{5,4},{6,7},{7,6},{8,9},{9,8},{10,11... | collective-permute-start | bytes 1572872 | tf_op jit(solution)/shard_map/ppermute | solution.py:45
  9.2 11.9 %collective-permute-done = bf16[1024,256]{1,0:T(8,128)(2,1)S(1)} collective-permute-done((bf16[1024,256]{1,0:T(8,128)(2,1)S(1)}, bf16[1024,256]{1,0:T(8,128)(2,1)S(1)}, u32[]{:S(2)}, u32[]{:S(2)}) %collective-permute-start) | collective-permute-done | bytes 524320 | tf_op jit(solution)/shard_map/ppermute | solution.py:45
  21.9 3.5 %fusion.12 = f32[256,2048]{1,0:T(8,128)S(1)} fusion(bf16[1024,2048]{1,0:T(8,128)(2,1)} %param.7, bf16[1024,256]{1,0:T(8,128)(2,1)S(1)} %collective-permute-done, bf16[2,1024,256]{2,1,0:T(8,128)(2,1)S(1)} %bitcast.195, s32[]{:T(128)S(6)} %select_n.196), kind=kOutput, calls=%fused_computation.42 | convolution fusion | flops 1074790400 | bytes 7340036 | tf_op jit(solution)/shard_map/dot_general | solution.py:29
  25.4 2.5 %fusion.3 = f32[2048,256]{0,1:T(8,128)S(1)} fusion(f32[256,2048]{1,0:T(8,128)S(1)} %fusion.12, bf16[1024,2048]{1,0:T(8,128)(2,1)S(1)} %copy-done.3, bf16[1024,256]{1,0:T(8,128)(2,1)} %copy-done.8, bf16[2,1024,256]{2,1,0:T(8,128)(2,1)} %bitcast.196, s32[]{:T(128)S(6)} %select_n.196), kind=kOutput, calls=%fused_computation.7 | convolution fusion | flops 1074528256 | bytes 9437188 | tf_op jit(solution)/shard_map/dot_general | solution.py:29
  27.9 3.0 %reshape.30 = f32[2,2,2,2,128,256]{4,3,2,1,0,5:T(2,128)} reshape(f32[2048,256]{0,1:T(8,128)S(1)} %fusion.3) | data formatting | bytes 4194304 | tf_op jit(solution)/shard_map/reshape | solution.py:53
  30.9 4.4 %constant_dynamic-slice_fusion.1 = (f32[2,2,2,1,128,256]{4,3,2,1,0,5:T(1,128)S(1)}, f32[2,2,2,1,128,256]{4,3,2,1,0,5:T(1,128)S(1)}) fusion(f32[2,2,2,2,128,256]{4,3,2,1,0,5:T(2,128)} %reshape.30, s32[]{:T(128)S(6)} %select_n.198, s32[]{:T(128)S(6)} %select_n.199), kind=kLoop, calls=%fused_computation.141 | loop fusion | bytes 4194312 | tf_op jit(solution)/shard_map/jit(dynamic_index_in_dim)/dynamic_slice | solution.py:58
  35.2 2.4 %copy.44 = f32[2,2,2,1,128,256]{5,4,1,0,2,3:T(8,128)} copy(f32[2,2,2,1,128,256]{4,3,2,1,0,5:T(1,128)S(1)} %get-tuple-element.31) | data formatting | bytes 2097152 | tf_op jit(solution)/shard_map/jit(dynamic_index_in_dim)/dynamic_slice | solution.py:59
  37.6 1.3 copy.43
  39.0 1.7 collective-permute-done.1
  40.6 1.4 bitcast_add_fusion.2
  42.0 1.8 collective-permute-start.2
  43.8 12.3 %collective-permute-done.2 = f32[2,2,128,256]{3,2,1,0:T(8,128)S(1)} collective-permute-done((f32[2,2,128,256]{3,2,1,0:T(8,128)S(1)}, f32[2,2,128,256]{3,2,1,0:T(8,128)S(1)}, u32[]{:S(2)}, u32[]{:S(2)}) %collective-permute-start.2) | collective-permute-done | bytes 524320 | tf_op jit(solution)/shard_map/ppermute | solution.py:45
  56.2 1.9 collective-permute-start.3
  58.0 5.8 %collective-permute-done.3 = f32[2,128,256]{2,1,0:T(8,128)S(1)} collective-permute-done((f32[2,128,256]{2,1,0:T(8,128)S(1)}, f32[2,128,256]{2,1,0:T(8,128)S(1)}, u32[]{:S(2)}, u32[]{:S(2)}) %collective-permute-start.3) | collective-permute-done | bytes 262176 | tf_op jit(solution)/shard_map/ppermute | solution.py:45
  63.9 2.8 %collective-permute-start.4 = (f32[128,256]{1,0:T(8,128)S(1)}, f32[128,256]{1,0:T(8,128)S(1)}, u32[]{:S(2)}, u32[]{:S(2)}) collective-permute-start(f32[128,256]{1,0:T(8,128)S(1)} %dynamic-slice_bitcast_fusion.6), channel_id=1, source_target_pairs={{0,16},{2,18},{4,20},{6,22},{8,24},{10,26},{12,28},{14,30},{16,0},... | collective-permute-start | bytes 393224 | tf_op jit(solution)/shard_map/ppermute | solution.py:45
  66.7 4.9 %collective-permute-done.4 = f32[128,256]{1,0:T(8,128)S(1)} collective-permute-done((f32[128,256]{1,0:T(8,128)S(1)}, f32[128,256]{1,0:T(8,128)S(1)}, u32[]{:S(2)}, u32[]{:S(2)}) %collective-permute-start.4) | collective-permute-done | bytes 131104 | tf_op jit(solution)/shard_map/ppermute | solution.py:45
  71.6 1.6 collective-permute-start.5
  73.4 3.2 %collective-permute-done.5 = f32[128,256]{1,0:T(8,128)S(1)} collective-permute-done((f32[128,256]{1,0:T(8,128)S(1)}, f32[128,256]{1,0:T(8,128)S(1)}, u32[]{:S(2)}, u32[]{:S(2)}) %collective-permute-start.5) | collective-permute-done | bytes 131104 | tf_op jit(solution)/shard_map/ppermute | solution.py:45
  77.4 1.1 collective-permute-start.10
  78.4 6.3 %collective-permute-done.10 = f32[128,256]{1,0:T(8,128)S(1)} collective-permute-done((f32[128,256]{1,0:T(8,128)S(1)}, f32[128,256]{1,0:T(8,128)S(1)}, u32[]{:S(2)}, u32[]{:S(2)}) %collective-permute-start.10) | collective-permute-done | bytes 131104 | tf_op jit(solution)/shard_map/ppermute | solution.py:45
  84.9 6.4 %collective-permute-done.11 = f32[2,128,256]{2,1,0:T(8,128)S(1)} collective-permute-done((f32[2,128,256]{2,1,0:T(8,128)S(1)}, f32[2,128,256]{2,1,0:T(8,128)S(1)}, u32[]{:S(2)}, u32[]{:S(2)}) %collective-permute-start.11) | collective-permute-done | bytes 262176 | tf_op jit(solution)/shard_map/ppermute | solution.py:45
  91.3 1.6 collective-permute-start.12
  92.9 7.6 %collective-permute-done.12 = f32[2,2,128,256]{3,2,1,0:T(8,128)S(1)} collective-permute-done((f32[2,2,128,256]{3,2,1,0:T(8,128)S(1)}, f32[2,2,128,256]{3,2,1,0:T(8,128)S(1)}, u32[]{:S(2)}, u32[]{:S(2)}) %collective-permute-start.12) | collective-permute-done | bytes 524320 | tf_op jit(solution)/shard_map/ppermute | solution.py:45
  100.7 1.1 pad_maximum_fusion.3
  101.8 2.9 %collective-permute-done.13 = f32[2,2,2,128,256]{4,3,2,1,0:T(8,128)S(1)} collective-permute-done((f32[2,2,2,128,256]{4,3,2,1,0:T(8,128)}, f32[2,2,2,128,256]{4,3,2,1,0:T(8,128)S(1)}, u32[]{:S(2)}, u32[]{:S(2)}) %collective-permute-start.13) | collective-permute-done | bytes 1048608 | tf_op jit(solution)/shard_map/ppermute | solution.py:45
  105.4 1.7 copy-done.4
  107.2 1.3 fusion.104
  108.5 1.3 fusion.9
  109.8 1.6 collective-permute-start.14
  111.4 1.1 collective-permute-start.6
  112.6 7.8 %collective-permute-done.6 = f32[128,256]{1,0:T(8,128)S(1)} collective-permute-done((f32[128,256]{1,0:T(8,128)S(1)}, f32[128,256]{1,0:T(8,128)S(1)}, u32[]{:S(2)}, u32[]{:S(2)}) %collective-permute-start.6) | collective-permute-done | bytes 131104 | tf_op jit(solution)/shard_map/ppermute | solution.py:45
  121.2 2.7 %collective-permute-done.14 = bf16[1024,256]{0,1:T(8,128)(2,1)S(1)} collective-permute-done((bf16[1024,256]{0,1:T(8,128)(2,1)S(1)}, bf16[1024,256]{0,1:T(8,128)(2,1)S(1)}, u32[]{:S(2)}, u32[]{:S(2)}) %collective-permute-start.14) | collective-permute-done | bytes 524320 | tf_op jit(solution)/shard_map/ppermute | solution.py:45
  124.8 3.6 %fusion.105 = f32[256,1024]{1,0:T(8,128)S(1)} fusion(bf16[2048,256]{1,0:T(8,128)(2,1)S(1)} %bitcast.198, bf16[2048,1024]{1,0:T(8,128)(2,1)} %param.6), kind=kOutput, calls=%fused_computation.186 | convolution fusion | flops 1073741824 | bytes 6291456 | tf_op jit(solution)/shard_map/dot_general | solution.py:29
  128.4 2.3 %fusion.7 = f32[1024,256]{0,1:T(8,128)} fusion(f32[256,1024]{1,0:T(8,128)S(1)} %fusion.105, bf16[2048,1024]{1,0:T(8,128)(2,1)S(1)} %copy-done.2, bf16[2048,256]{1,0:T(8,128)(2,1)S(1)} %bitcast.199), kind=kOutput, calls=%fused_computation.19 | convolution fusion | flops 1075576832 | bytes 7340032 | tf_op jit(solution)/shard_map/dot_general | solution.py:29
  130.7 1.6 copy.56
  132.4 1.0 select_bitcast_fusion.17
  133.4 1.6 collective-permute-start.8
  135.2 0.8 collective-permute-start.16
  136.0 12.3 %collective-permute-done.8 = f32[2,2,128,256]{3,2,1,0:T(8,128)S(1)} collective-permute-done((f32[2,2,128,256]{3,2,1,0:T(8,128)S(1)}, f32[2,2,128,256]{3,2,1,0:T(8,128)S(1)}, u32[]{:S(2)}, u32[]{:S(2)}) %collective-permute-start.8) | collective-permute-done | bytes 524320 | tf_op jit(solution)/shard_map/ppermute | solution.py:45
  148.4 1.1 pad_maximum_fusion.2
  149.5 3.9 %collective-permute-done.16 = f32[2,2,64,256]{3,2,1,0:T(8,128)S(1)} collective-permute-done((f32[2,2,64,256]{3,2,1,0:T(8,128)S(1)}, f32[2,2,64,256]{3,2,1,0:T(8,128)S(1)}, u32[]{:S(2)}, u32[]{:S(2)}) %collective-permute-start.16) | collective-permute-done | bytes 262176 | tf_op jit(solution)/shard_map/ppermute | solution.py:45
  153.6 5.0 %collective-permute-done.17 = f32[2,64,256]{2,1,0:T(8,128)S(1)} collective-permute-done((f32[2,64,256]{2,1,0:T(8,128)S(1)}, f32[2,64,256]{2,1,0:T(8,128)S(1)}, u32[]{:S(2)}, u32[]{:S(2)}) %collective-permute-start.17) | collective-permute-done | bytes 131104 | tf_op jit(solution)/shard_map/ppermute | solution.py:45
  159.3 1.6 collective-permute-start.18
  160.9 6.4 %copy.40 = bf16[1024,2048]{0,1:T(8,128)(2,1)} copy(bf16[1024,2048]{1,0:T(8,128)(2,1)} %param.8) | data formatting | bytes 8388608 | tf_op args[2]
  168.8 0.8 bitcast_add_fusion.12
  169.7 1.3 collective-permute-start.19
  171.2 3.7 %collective-permute-done.19 = f32[64,256]{1,0:T(8,128)S(1)} collective-permute-done((f32[64,256]{1,0:T(8,128)S(1)}, f32[64,256]{1,0:T(8,128)S(1)}, u32[]{:S(2)}, u32[]{:S(2)}) %collective-permute-start.19) | collective-permute-done | bytes 65568 | tf_op jit(solution)/shard_map/ppermute | solution.py:45
  174.9 2.2 %collective-permute-start.20 = (f32[2,64,256]{2,1,0:T(8,128)S(1)}, f32[2,64,256]{2,1,0:T(8,128)S(1)}, u32[]{:S(2)}, u32[]{:S(2)}) collective-permute-start(f32[2,64,256]{2,1,0:T(8,128)S(1)} %pad_maximum_fusion.13), channel_id=1, source_target_pairs={{0,8},{2,10},{4,12},{6,14},{8,0},{10,2},{12,4},{14,6},{16,24},{18,... | collective-permute-start | bytes 393224 | tf_op jit(solution)/shard_map/ppermute | solution.py:45
  177.3 2.8 %collective-permute-done.20 = f32[2,64,256]{2,1,0:T(8,128)S(1)} collective-permute-done((f32[2,64,256]{2,1,0:T(8,128)S(1)}, f32[2,64,256]{2,1,0:T(8,128)S(1)}, u32[]{:S(2)}, u32[]{:S(2)}) %collective-permute-start.20) | collective-permute-done | bytes 131104 | tf_op jit(solution)/shard_map/ppermute | solution.py:45
  180.1 1.5 collective-permute-start.21
  181.9 4.6 %collective-permute-done.21 = f32[2,2,64,256]{3,2,1,0:T(8,128)S(1)} collective-permute-done((f32[2,2,64,256]{3,2,1,0:T(8,128)S(1)}, f32[2,2,64,256]{3,2,1,0:T(8,128)S(1)}, u32[]{:S(2)}, u32[]{:S(2)}) %collective-permute-start.21) | collective-permute-done | bytes 262176 | tf_op jit(solution)/shard_map/ppermute | solution.py:45
  186.7 1.3 fusion.94
  188.0 1.3 fusion.97
  190.2 2.6 %convolution_bitcast_fusion.1 = f32[256,256]{1,0:T(8,128)} fusion(f32[2,2,2,1,64,256]{5,4,3,2,1,0:T(8,128)S(1)} %get-tuple-element.33, f32[2,2,2,1,64,256]{5,4,3,2,1,0:T(8,128)S(1)} %get-tuple-element.32), kind=kOutput, calls=%fused_computation.25 | convolution fusion | flops 805568512 | bytes 1310720 | tf_op jit(solution)/shard_map/dot_general | solution.py:121
  192.8 1.5 collective-permute-start.23
  194.3 6.2 %fusion.1 = bf16[1024,2048]{0,1:T(8,128)(2,1)} fusion(f32[1024,2048]{0,1:T(8,128)S(1)} %fusion.94, f32[2048,1024]{1,0:T(8,128)S(1)} %fusion.97, bf16[1024,2048]{0,1:T(8,128)(2,1)} %copy.40, bf16[2048,256]{1,0:T(8,128)(2,1)S(1)} %get-tuple-element.20, f32[1024,256]{1,0:T(8,128)S(1)} %copy-done), kind=kOutput, calls=%fused_computation.2 | convolution fusion | flops 1084489728 | bytes 27262976 | tf_op jit(solution)/shard_map/dot_general | solution.py:139
  200.5 6.4 %copy.60 = bf16[1024,2048]{1,0:T(8,128)(2,1)} copy(bf16[1024,2048]{0,1:T(8,128)(2,1)} %fusion.1) | data formatting | bytes 8388608
  206.9 1.8 select_reduce_fusion
  209.4 1.1 fusion.17
  210.4 1.0 fusion.16
  211.5 1.1 fusion.15
  216.3 2.0 fusion.107
  (92 shorter events, 12.9 us)
Async XLA Ops:
  0.6 4.0 %copy-start.1 = (bf16[2048,1024]{1,0:T(8,128)(2,1)S(1)}, bf16[2048,1024]{1,0:T(8,128)(2,1)}, u32[]{:S(2)}) copy-start(bf16[2048,1024]{1,0:T(8,128)(2,1)} %param.6) | copy-start | bytes 12582916
  0.6 4.0 %copy-start = (f32[1024,256]{1,0:T(8,128)S(1)}, f32[1024,256]{1,0:T(8,128)}, u32[]{:S(2)}) copy-start(f32[1024,256]{1,0:T(8,128)} %param.9) | copy-start | bytes 3145732
  6.0 15.1 %copy-start.7 = (bf16[2048,256]{1,0:T(8,128)(2,1)}, bf16[2048,256]{1,0:T(8,128)(2,1)S(1)}, u32[]{:S(2)}) copy-start(bf16[2048,256]{1,0:T(8,128)(2,1)S(1)} %fusion.4) | copy-start | bytes 3145732
  6.1 15.0 %collective-permute-start = (bf16[1024,256]{1,0:T(8,128)(2,1)S(1)}, bf16[1024,256]{1,0:T(8,128)(2,1)S(1)}, u32[]{:S(2)}, u32[]{:S(2)}) collective-permute-start(bf16[1024,256]{1,0:T(8,128)(2,1)S(1)} %dynamic-slice_bitcast_fusion.2), channel_id=1, source_target_pairs={{0,1},{1,0},{2,3},{3,2},{4,5},{5,4},{6,7},{7,6},{8,9},{9,8},{10,11... | collective-permute-start | bytes 1572872 | tf_op jit(solution)/shard_map/ppermute | solution.py:45
  9.2 16.2 %copy-start.3 = (bf16[1024,2048]{1,0:T(8,128)(2,1)S(1)}, bf16[1024,2048]{1,0:T(8,128)(2,1)}, u32[]{:S(2)}) copy-start(bf16[1024,2048]{1,0:T(8,128)(2,1)} %param.7) | copy-start | bytes 12582916
  21.1 0.8 copy-start.8
  37.6 3.0 %collective-permute-start.1 = (f32[2,2,2,128,256]{4,3,1,0,2:T(8,128)}, f32[2,2,2,128,256]{4,3,1,0,2:T(8,128)}, u32[]{:S(2)}, u32[]{:S(2)}) collective-permute-start(f32[2,2,2,128,256]{4,3,1,0,2:T(8,128)} %bitcast.197), channel_id=1, source_target_pairs={{0,2},{2,0},{4,6},{6,4},{8,10},{10,8},{12,14},{14,12},{16,18},{18,... | collective-permute-start | bytes 3145736 | tf_op jit(solution)/shard_map/ppermute | solution.py:45
  38.9 34.3 %copy-start.10 = (f32[256,128]{1,0:T(8,128)S(1)}, f32[256,128]{1,0:T(8,128)}, u32[]{:S(2)}) copy-start(f32[256,128]{1,0:T(8,128)} %param.10) | copy-start | bytes 393220
  39.0 34.4 %copy-start.11 = (f32[256,128]{1,0:T(8,128)S(1)}, f32[256,128]{1,0:T(8,128)}, u32[]{:S(2)}) copy-start(f32[256,128]{1,0:T(8,128)} %param.11) | copy-start | bytes 393220
  42.0 14.0 %collective-permute-start.2 = (f32[2,2,128,256]{3,2,1,0:T(8,128)S(1)}, f32[2,2,128,256]{3,2,1,0:T(8,128)S(1)}, u32[]{:S(2)}, u32[]{:S(2)}) collective-permute-start(f32[2,2,128,256]{3,2,1,0:T(8,128)S(1)} %dynamic-slice_bitcast_fusion.1), channel_id=1, source_target_pairs={{0,4},{2,6},{4,0},{6,2},{8,12},{10,14},{12,8},{14,10},{16,20},{18,... | collective-permute-start | bytes 1572872 | tf_op jit(solution)/shard_map/ppermute | solution.py:45
  56.2 7.6 %collective-permute-start.3 = (f32[2,128,256]{2,1,0:T(8,128)S(1)}, f32[2,128,256]{2,1,0:T(8,128)S(1)}, u32[]{:S(2)}, u32[]{:S(2)}) collective-permute-start(f32[2,128,256]{2,1,0:T(8,128)S(1)} %dynamic-slice_bitcast_fusion.4), channel_id=1, source_target_pairs={{0,8},{2,10},{4,12},{6,14},{8,0},{10,2},{12,4},{14,6},{16,24},{18,... | collective-permute-start | bytes 786440 | tf_op jit(solution)/shard_map/ppermute | solution.py:45
  63.9 7.7 %collective-permute-start.4 = (f32[128,256]{1,0:T(8,128)S(1)}, f32[128,256]{1,0:T(8,128)S(1)}, u32[]{:S(2)}, u32[]{:S(2)}) collective-permute-start(f32[128,256]{1,0:T(8,128)S(1)} %dynamic-slice_bitcast_fusion.6), channel_id=1, source_target_pairs={{0,16},{2,18},{4,20},{6,22},{8,24},{10,26},{12,28},{14,30},{16,0},... | collective-permute-start | bytes 393224 | tf_op jit(solution)/shard_map/ppermute | solution.py:45
  71.6 5.0 %collective-permute-start.5 = (f32[128,256]{1,0:T(8,128)S(1)}, f32[128,256]{1,0:T(8,128)S(1)}, u32[]{:S(2)}, u32[]{:S(2)}) collective-permute-start(f32[128,256]{1,0:T(8,128)S(1)} %bitcast_add_fusion.11), channel_id=1, source_target_pairs={{0,1},{1,0},{2,3},{3,2},{4,5},{5,4},{6,7},{7,6},{8,9},{9,8},{10,11... | collective-permute-start | bytes 393224 | tf_op jit(solution)/shard_map/ppermute | solution.py:45
  77.4 7.4 %collective-permute-start.10 = (f32[128,256]{1,0:T(8,128)S(1)}, f32[128,256]{1,0:T(8,128)S(1)}, u32[]{:S(2)}, u32[]{:S(2)}) collective-permute-start(f32[128,256]{1,0:T(8,128)S(1)} %get-tuple-element.25), channel_id=1, source_target_pairs={{0,16},{2,18},{4,20},{6,22},{8,24},{10,26},{12,28},{14,30},{16,0},... | collective-permute-start | bytes 393224 | tf_op jit(solution)/shard_map/ppermute | solution.py:45
  84.8 6.4 %collective-permute-start.11 = (f32[2,128,256]{2,1,0:T(8,128)S(1)}, f32[2,128,256]{2,1,0:T(8,128)S(1)}, u32[]{:S(2)}, u32[]{:S(2)}) collective-permute-start(f32[2,128,256]{2,1,0:T(8,128)S(1)} %pad_maximum_fusion.11), channel_id=1, source_target_pairs={{0,8},{2,10},{4,12},{6,14},{8,0},{10,2},{12,4},{14,6},{16,24},{18,... | collective-permute-start | bytes 786440 | tf_op jit(solution)/shard_map/ppermute | solution.py:45
  91.3 9.2 %collective-permute-start.12 = (f32[2,2,128,256]{3,2,1,0:T(8,128)S(1)}, f32[2,2,128,256]{3,2,1,0:T(8,128)S(1)}, u32[]{:S(2)}, u32[]{:S(2)}) collective-permute-start(f32[2,2,128,256]{3,2,1,0:T(8,128)S(1)} %pad_maximum_fusion.8), channel_id=1, source_target_pairs={{0,4},{2,6},{4,0},{6,2},{8,12},{10,14},{12,8},{14,10},{16,20},{18,... | collective-permute-start | bytes 1572872 | tf_op jit(solution)/shard_map/ppermute | solution.py:45
  101.8 2.9 %collective-permute-start.13 = (f32[2,2,2,128,256]{4,3,2,1,0:T(8,128)}, f32[2,2,2,128,256]{4,3,2,1,0:T(8,128)S(1)}, u32[]{:S(2)}, u32[]{:S(2)}) collective-permute-start(f32[2,2,2,128,256]{4,3,2,1,0:T(8,128)} %pad_maximum_fusion.3), channel_id=1, source_target_pairs={{0,2},{2,0},{4,6},{6,4},{8,10},{10,8},{12,14},{14,12},{16,18},{18,... | collective-permute-start | bytes 3145736 | tf_op jit(solution)/shard_map/ppermute | solution.py:45
  105.0 2.2 %copy-start.4 = (bf16[1024,2048]{1,0:T(8,128)(2,1)S(1)}, bf16[1024,2048]{1,0:T(8,128)(2,1)}, u32[]{:S(2)}) copy-start(bf16[1024,2048]{1,0:T(8,128)(2,1)} %param.7) | copy-start | bytes 12582916
  109.8 14.0 %collective-permute-start.14 = (bf16[1024,256]{0,1:T(8,128)(2,1)S(1)}, bf16[1024,256]{0,1:T(8,128)(2,1)S(1)}, u32[]{:S(2)}, u32[]{:S(2)}) collective-permute-start(bf16[1024,256]{0,1:T(8,128)(2,1)S(1)} %fusion.9), channel_id=1, source_target_pairs={{0,1},{1,0},{2,3},{3,2},{4,5},{5,4},{6,7},{7,6},{8,9},{9,8},{10,11... | collective-permute-start | bytes 1572872 | tf_op jit(solution)/shard_map/ppermute | solution.py:45
  111.4 9.0 %collective-permute-start.6 = (f32[128,256]{1,0:T(8,128)S(1)}, f32[128,256]{1,0:T(8,128)S(1)}, u32[]{:S(2)}, u32[]{:S(2)}) collective-permute-start(f32[128,256]{1,0:T(8,128)S(1)} %get-tuple-element.22), channel_id=1, source_target_pairs={{0,16},{2,18},{4,20},{6,22},{8,24},{10,26},{12,28},{14,30},{16,0},... | collective-permute-start | bytes 393224 | tf_op jit(solution)/shard_map/ppermute | solution.py:45
  121.2 11.2 %collective-permute-start.7 = (f32[2,128,256]{2,1,0:T(8,128)}, f32[2,128,256]{2,1,0:T(8,128)}, u32[]{:S(2)}, u32[]{:S(2)}) collective-permute-start(f32[2,128,256]{2,1,0:T(8,128)} %pad_maximum_fusion.10), channel_id=1, source_target_pairs={{0,8},{2,10},{4,12},{6,14},{8,0},{10,2},{12,4},{14,6},{16,24},{18,... | collective-permute-start | bytes 786440 | tf_op jit(solution)/shard_map/ppermute | solution.py:45
  124.8 3.6 %copy-start.2 = (bf16[2048,1024]{1,0:T(8,128)(2,1)S(1)}, bf16[2048,1024]{1,0:T(8,128)(2,1)}, u32[]{:S(2)}) copy-start(bf16[2048,1024]{1,0:T(8,128)(2,1)} %param.6) | copy-start | bytes 12582916
  132.3 2.7 %collective-permute-start.15 = (f32[2,2,2,64,256]{4,3,2,1,0:T(8,128)S(1)}, f32[2,2,2,64,256]{4,3,2,1,0:T(8,128)S(1)}, u32[]{:S(2)}, u32[]{:S(2)}) collective-permute-start(f32[2,2,2,64,256]{4,3,2,1,0:T(8,128)S(1)} %dynamic-slice_bitcast_fusion), channel_id=1, source_target_pairs={{0,2},{2,0},{4,6},{6,4},{8,10},{10,8},{12,14},{14,12},{16,18},{18,... | collective-permute-start | bytes 1572872 | tf_op jit(solution)/shard_map/ppermute | solution.py:45
  133.4 14.9 %collective-permute-start.8 = (f32[2,2,128,256]{3,2,1,0:T(8,128)S(1)}, f32[2,2,128,256]{3,2,1,0:T(8,128)S(1)}, u32[]{:S(2)}, u32[]{:S(2)}) collective-permute-start(f32[2,2,128,256]{3,2,1,0:T(8,128)S(1)} %pad_maximum_fusion.7), channel_id=1, source_target_pairs={{0,4},{2,6},{4,0},{6,2},{8,12},{10,14},{12,8},{14,10},{16,20},{18,... | collective-permute-start | bytes 1572872 | tf_op jit(solution)/shard_map/ppermute | solution.py:45
  135.2 18.3 %collective-permute-start.16 = (f32[2,2,64,256]{3,2,1,0:T(8,128)S(1)}, f32[2,2,64,256]{3,2,1,0:T(8,128)S(1)}, u32[]{:S(2)}, u32[]{:S(2)}) collective-permute-start(f32[2,2,64,256]{3,2,1,0:T(8,128)S(1)} %dynamic-slice_bitcast_fusion.3), channel_id=1, source_target_pairs={{0,4},{2,6},{4,0},{6,2},{8,12},{10,14},{12,8},{14,10},{16,20},{18,... | collective-permute-start | bytes 786440 | tf_op jit(solution)/shard_map/ppermute | solution.py:45
  149.5 21.5 %collective-permute-start.9 = (f32[2,2,2,128,256]{4,3,2,1,0:T(8,128)}, f32[2,2,2,128,256]{4,3,2,1,0:T(8,128)S(1)}, u32[]{:S(2)}, u32[]{:S(2)}) collective-permute-start(f32[2,2,2,128,256]{4,3,2,1,0:T(8,128)} %pad_maximum_fusion.2), channel_id=1, source_target_pairs={{0,2},{2,0},{4,6},{6,4},{8,10},{10,8},{12,14},{14,12},{16,18},{18,... | collective-permute-start | bytes 3145736 | tf_op jit(solution)/shard_map/ppermute | solution.py:45
  153.5 5.1 %collective-permute-start.17 = (f32[2,64,256]{2,1,0:T(8,128)S(1)}, f32[2,64,256]{2,1,0:T(8,128)S(1)}, u32[]{:S(2)}, u32[]{:S(2)}) collective-permute-start(f32[2,64,256]{2,1,0:T(8,128)S(1)} %dynamic-slice_bitcast_fusion.5), channel_id=1, source_target_pairs={{0,8},{2,10},{4,12},{6,14},{8,0},{10,2},{12,4},{14,6},{16,24},{18,... | collective-permute-start | bytes 393224 | tf_op jit(solution)/shard_map/ppermute | solution.py:45
  159.3 8.0 %copy-start.9 = (f32[256,128]{0,1:T(8,128)S(1)}, f32[256,128]{0,1:T(8,128)}, u32[]{:S(2)}) copy-start(f32[256,128]{0,1:T(8,128)} %get-tuple-element.23) | copy-start | bytes 393220
  159.3 9.6 %collective-permute-start.18 = (f32[64,256]{1,0:T(8,128)}, f32[64,256]{1,0:T(8,128)}, u32[]{:S(2)}, u32[]{:S(2)}) collective-permute-start(f32[64,256]{1,0:T(8,128)} %dynamic-slice_bitcast_fusion.7), channel_id=1, source_target_pairs={{0,16},{2,18},{4,20},{6,22},{8,24},{10,26},{12,28},{14,30},{16,0},... | collective-permute-start | bytes 196616 | tf_op jit(solution)/shard_map/ppermute | solution.py:45
  169.7 5.2 %collective-permute-start.19 = (f32[64,256]{1,0:T(8,128)S(1)}, f32[64,256]{1,0:T(8,128)S(1)}, u32[]{:S(2)}, u32[]{:S(2)}) collective-permute-start(f32[64,256]{1,0:T(8,128)S(1)} %bitcast_add_fusion.12), channel_id=1, source_target_pairs={{0,16},{2,18},{4,20},{6,22},{8,24},{10,26},{12,28},{14,30},{16,0},... | collective-permute-start | bytes 196616 | tf_op jit(solution)/shard_map/ppermute | solution.py:45
  174.9 5.2 %collective-permute-start.20 = (f32[2,64,256]{2,1,0:T(8,128)S(1)}, f32[2,64,256]{2,1,0:T(8,128)S(1)}, u32[]{:S(2)}, u32[]{:S(2)}) collective-permute-start(f32[2,64,256]{2,1,0:T(8,128)S(1)} %pad_maximum_fusion.13), channel_id=1, source_target_pairs={{0,8},{2,10},{4,12},{6,14},{8,0},{10,2},{12,4},{14,6},{16,24},{18,... | collective-permute-start | bytes 393224 | tf_op jit(solution)/shard_map/ppermute | solution.py:45
  180.1 6.4 %collective-permute-start.21 = (f32[2,2,64,256]{3,2,1,0:T(8,128)S(1)}, f32[2,2,64,256]{3,2,1,0:T(8,128)S(1)}, u32[]{:S(2)}, u32[]{:S(2)}) collective-permute-start(f32[2,2,64,256]{3,2,1,0:T(8,128)S(1)} %pad_maximum_fusion.12), channel_id=1, source_target_pairs={{0,4},{2,6},{4,0},{6,2},{8,12},{10,14},{12,8},{14,10},{16,20},{18,... | collective-permute-start | bytes 786440 | tf_op jit(solution)/shard_map/ppermute | solution.py:45
  186.7 2.7 %collective-permute-start.22 = (f32[2,2,2,64,256]{4,3,2,1,0:T(8,128)S(1)}, f32[2,2,2,64,256]{4,3,2,1,0:T(8,128)S(1)}, u32[]{:S(2)}, u32[]{:S(2)}) collective-permute-start(f32[2,2,2,64,256]{4,3,2,1,0:T(8,128)S(1)} %pad_maximum_fusion.9), channel_id=1, source_target_pairs={{0,2},{2,0},{4,6},{6,4},{8,10},{10,8},{12,14},{14,12},{16,18},{18,... | collective-permute-start | bytes 1572872 | tf_op jit(solution)/shard_map/ppermute | solution.py:45
  189.4 0.8 copy-start.5
  192.8 14.1 %collective-permute-start.23 = (f32[256,256]{1,0:T(8,128)}, f32[256,256]{1,0:T(8,128)}, u32[]{:S(2)}, u32[]{:S(2)}) collective-permute-start(f32[256,256]{1,0:T(8,128)} %convolution_bitcast_fusion.1), channel_id=1, source_target_pairs={{0,1},{1,0},{2,3},{3,2},{4,5},{5,4},{6,7},{7,6},{8,9},{9,8},{10,11... | collective-permute-start | bytes 786440 | tf_op jit(solution)/shard_map/ppermute | solution.py:45
  206.9 6.0 %copy-start.6 = (f32[2,2,2,1,64,256]{5,4,3,2,1,0:T(8,128)S(1)}, f32[2,2,2,1,64,256]{5,4,3,2,1,0:T(8,128)}, u32[]{:S(2)}) copy-start(f32[2,2,2,1,64,256]{5,4,3,2,1,0:T(8,128)} %copy-done.5) | copy-start | bytes 1572868
